TPU v7x, 128 devices: a whole 4x4x4 slice. The times are simulated.
128 devices in a mesh: seq: 64 (over y, x, z), head: 2 (over core).
Axes of the slice: x: 4, y: 4, z: 4, core: 2. Of those that a mesh axis runs over, the one named last changes fastest.
Arguments:
- x_in: bfloat16 [32768, 4096], P('seq', 'head'), may hold values from -6 to 6
- gate_input: bfloat16 [32768, 4096], P('seq', 'head'), may hold values from -6 to 6
- in_b: bfloat16 [32768, 512], P('seq', 'head'), may hold values from -2 to 2
- in_c: bfloat16 [32768, 512], P('seq', 'head'), may hold values from -2 to 2
- step_size: float32 [32768, 64], P('seq', 'head'), may hold values from 0.02 to 0.2
- log_decay: float32 [32768, 64], P('seq', 'head'), may hold values from -0.7 to 0, as said below
- skip_gain: float32 [64], P('head'), may hold values from 0.5 to 1.5
- norm_gain: float32 [4096], P('head'), may hold values from 0.5 to 1.5
- out_weight: bfloat16 [4096, 8192], P('head', 'seq'), may hold values from -0.046875 to 0.046875
- probe: bfloat16 [64, 8192, 128], P('seq', 'head'), may hold values from -0.29882812 to 0.29882812
- span_start: int32 [4096], P('seq'), may hold values from 0 to 32767, as said below
- span_len: int32 [4096], P('seq'), may hold values from 1 to 128, as said below
- span_owner: int32 [4096, 1], P('seq'), may hold values from 0 to 63; in each aligned block of 64 rows (0 to 63, 64 to 127, ...) at most 2 rows name the same one
- span_label: int32 [4096], P('seq'), may hold values from 0 to 127
Outputs:
- layer_out: bfloat16 [32768, 8192], P('seq', 'head')
- probe_grad: float32 [64, 8192, 128], P('seq', 'head')
- slot_loss: float32 [64, 128], P('seq')
Inputs may be any that keep to these rules, and one draw needn't show every extreme that they name: `log_decay`: log of a decay factor in (0, 1]. Span i starts among tokens (i // 64) * 512 to (i // 64 + 1) * 512 - 1, and span_start + span_len <= 32768. `span_len`: the first span of every block of 64 spans is 128 long. `span_owner`: in each aligned block of 64 spans no owner appears more than 2 times.
All inputs are finite; a program needn't handle non-finite values.
Results may differ from a plain program's by a relative error of at most 0.0068.
Values may be sent and summed in bfloat16 or wider, within the bound.
No kernel may reach another device: no remote copies, remote signals or barrier semaphores. Data moves between devices by JAX's collectives and lax.ppermute only.
A program may use at most 256 MiB of HBM per device.

v0:
```python
import jax
import jax.numpy as jnp
from jax import lax
from jax.sharding import PartitionSpec as P

HEAD_DIM = 64
STATE = 128
CAP = 2


def prefix(part, axis, combine, identity):
    place = lax.axis_index(axis)
    gathered = jax.tree.map(lambda a: lax.all_gather(a, axis), part)
    state = jax.tree.map(lambda a, e: jnp.zeros_like(a) + jnp.asarray(e, a.dtype), part, identity)

    def one(step, state):
        return combine(
            state, jax.tree.map(lambda a: lax.dynamic_index_in_dim(a, step, 0, False), gathered)
        )

    return lax.fori_loop(0, place, one, state)


def from_behind(value, axis, steps):
    count = lax.axis_size(axis)
    leading, last = (max(0, -steps), min(count, count - steps))
    return lax.ppermute(value, axis, [(source, source + steps) for source in range(leading, last)])


def segment_summands(xs, bmat, cmat, dtk, cum):
    high = lax.Precision.HIGHEST
    tok = xs.shape[0]
    cb = jnp.einsum("tgn,sgn->gts", cmat, bmat, precision=high)
    ordered = jnp.transpose(cum, (1, 2, 0))
    diff = ordered[:, :, :, None] - ordered[:, :, None, :]
    lower = jnp.arange(tok)[:, None] >= jnp.arange(tok)[None, :]
    decay = jnp.where(lower, jnp.exp(jnp.where(lower, diff, 0.0)), 0.0)
    weights = cb[:, None] * decay * jnp.transpose(dtk, (1, 2, 0))[:, :, None, :]
    intra = jnp.einsum("gkts,sgkp->tgkp", weights, xs, precision=high)
    tail = jnp.exp(cum[-1][None] - cum) * dtk
    local_state = jnp.einsum("tgk,tgkp,tgn->gkpn", tail, xs, bmat, precision=high)
    return (intra, local_state, cum[-1])


def inter_term(cmat, cum, state_in):
    high = lax.Precision.HIGHEST
    return jnp.exp(cum)[..., None] * jnp.einsum("tgn,gkpn->tgkp", cmat, state_in, precision=high)


def piecewise_terms(xs, bmat, cmat, dtk, logd):
    tok = xs.shape[0]
    width = min(tok, 256)
    pieces = tok // width
    state = jnp.zeros((xs.shape[1], xs.shape[2], xs.shape[3], bmat.shape[2]), jnp.float32)
    total = jnp.zeros((xs.shape[1], xs.shape[2]), jnp.float32)
    results = []
    for piece in range(pieces):
        lower_edge = piece * width
        upper_edge = lower_edge + width
        inner_cum = jnp.cumsum(logd[lower_edge:upper_edge], axis=0)
        intra, local_state, piece_total = segment_summands(
            xs[lower_edge:upper_edge],
            bmat[lower_edge:upper_edge],
            cmat[lower_edge:upper_edge],
            dtk[lower_edge:upper_edge],
            inner_cum,
        )
        results.append(intra + inter_term(cmat[lower_edge:upper_edge], inner_cum, state))
        state = state * jnp.exp(piece_total)[..., None, None] + local_state
        total = total + piece_total
    return (jnp.concatenate(results, axis=0), state, total)


def combine_states(earlier, later):
    return (earlier[0] * jnp.exp(later[1])[..., None, None] + later[0], earlier[1] + later[1])


def inside_mask(first, length, place):
    return jnp.logical_and(
        place[None, :] >= first[:, None], place[None, :] < (first + length)[:, None]
    ).astype(jnp.bfloat16)


def on_device(
    x_in,
    gate_input,
    in_b,
    in_c,
    step_size,
    log_decay,
    skip_gain,
    norm_gain,
    out_weight,
    probe,
    span_start,
    span_len,
    span_owner,
    span_label,
):
    tok = x_in.shape[0]
    local_attention_heads = step_size.shape[1]
    groups_here = in_b.shape[1] // STATE
    per_group = local_attention_heads // groups_here
    xs = x_in.astype(jnp.float32).reshape(tok, groups_here, per_group, HEAD_DIM)
    bmat = in_b.astype(jnp.float32).reshape(tok, groups_here, STATE)
    cmat = in_c.astype(jnp.float32).reshape(tok, groups_here, STATE)
    dtk = step_size.reshape(tok, groups_here, per_group)
    logd = log_decay.reshape(tok, groups_here, per_group)
    cum = jnp.cumsum(logd, axis=0)
    intra, local_state, total = piecewise_terms(xs, bmat, cmat, dtk, logd)
    identity = (jnp.zeros_like(local_state), jnp.zeros_like(total))
    state_in, unused = prefix((local_state, total), "seq", combine_states, identity)
    ssm = (
        intra
        + inter_term(cmat, cum, state_in)
        + skip_gain.reshape(groups_here, per_group)[None, :, :, None] * xs
    )
    ssm = ssm.reshape(tok, groups_here, per_group * HEAD_DIM)
    gated = ssm * jax.nn.silu(
        gate_input.astype(jnp.float32).reshape(tok, groups_here, per_group * HEAD_DIM)
    )
    meansq = jnp.mean(gated * gated, axis=-1, keepdims=True)
    normalized_input = gated * lax.rsqrt(meansq + 1e-05)
    y_out = (normalized_input.reshape(tok, -1) * norm_gain[None, :]).astype(jnp.bfloat16)
    partial_out = jnp.dot(
        y_out,
        lax.all_gather(out_weight, "seq", axis=1, tiled=True),
        preferred_element_type=jnp.float32,
    )
    layer_out = lax.psum_scatter(
        partial_out.astype(jnp.bfloat16), "head", scatter_dimension=1, tiled=True
    )
    base = lax.axis_index("seq") * tok
    prev_start, prev_len = from_behind((span_start, span_len), "seq", 1)
    place = base + jnp.arange(tok, dtype=jnp.int32)
    spill_sums = jnp.dot(
        inside_mask(prev_start, prev_len, place), layer_out, preferred_element_type=jnp.float32
    )
    returned = from_behind(spill_sums, "seq", -1)
    sums = (
        jnp.dot(
            inside_mask(span_start, span_len, place), layer_out, preferred_element_type=jnp.float32
        )
        + returned
    )
    count = span_start.shape[0]
    owners = lax.axis_size("seq")
    slots_total = owners * CAP
    owner = span_owner[:, 0]
    index = jnp.arange(count)
    earlier = index[None, :] < index[:, None]
    same = owner[:, None] == owner[None, :]
    slot = jnp.sum(jnp.logical_and(same, earlier), axis=1)
    target_labels = owner * CAP + slot
    pick = jnp.arange(slots_total, dtype=jnp.int32)[:, None] == target_labels[None, :]
    send_sums = jnp.dot(pick.astype(jnp.float32), sums, precision=lax.Precision.HIGHEST).reshape(
        owners, CAP, -1
    )
    label_slots = jnp.sum(jnp.where(pick, span_label[None, :] + 1, 0), axis=1) - 1
    length_slots = jnp.sum(jnp.where(pick, span_len[None, :], 0), axis=1)
    meta = jnp.stack([label_slots, length_slots], axis=-1).reshape(owners, CAP, 2)
    got_sums, got_meta = (
        lax.all_to_all(send_sums, "seq", split_axis=0, concat_axis=0, tiled=True),
        lax.all_to_all(meta, "seq", split_axis=0, concat_axis=0, tiled=True),
    )
    labels = got_meta[:, :, 0].reshape(-1)
    lengths = got_meta[:, :, 1].reshape(-1)
    valid = labels >= 0
    feature = (
        got_sums.reshape(slots_total, -1) / jnp.maximum(lengths, 1)[:, None].astype(jnp.float32)
    ).astype(jnp.bfloat16)
    partial_logits = jnp.dot(feature, probe[0], preferred_element_type=jnp.float32)
    logits = lax.psum(partial_logits, "head")
    top = jnp.max(logits, axis=1, keepdims=True)
    lse = top[:, 0] + jnp.log(jnp.sum(jnp.exp(logits - top), axis=1))
    onehot = jnp.arange(logits.shape[1])[None, :] == labels[:, None]
    picked = jnp.sum(jnp.where(onehot, logits, 0.0), axis=1)
    loss = jnp.where(valid, lse - picked, 0.0)
    probs = jnp.exp(logits - lse[:, None])
    resid = jnp.where(valid[:, None], probs - onehot.astype(jnp.float32), 0.0).astype(jnp.bfloat16)
    grad = jnp.dot(feature.T, resid, preferred_element_type=jnp.float32)
    return (layer_out, grad[None], loss[None])


def solution(mesh):
    placed = (
        P("seq", "head"),
        P("seq", "head"),
        P("seq", "head"),
        P("seq", "head"),
        P("seq", "head"),
        P("seq", "head"),
        P("head"),
        P("head"),
        P("head", "seq"),
        P("seq", "head", None),
        P("seq"),
        P("seq"),
        P("seq", None),
        P("seq"),
    )
    return jax.shard_map(
        on_device,
        mesh=mesh,
        in_specs=placed,
        out_specs=(P("seq", "head"), P("seq", "head", None), P("seq", None)),
        check_vma=False,
    )
```

profile of v0, /device:TPU:1, one launch (start us, length us, event | category | flops | bytes accessed | tf_op | source)
XLA Modules:
  0.0 707.1 jit_solution(5260263561562434642)
XLA Ops:
  8.1 1.2 reduce-window.24
  12.2 1.4 fusion.91
  15.5 2.7 fusion.87
  18.2 1.5 copy.150
  20.7 1.2 exp.75
  21.9 1.3 copy.160
  23.3 1.5 exponential_multiply_fusion
  24.9 1.8 fusion.41
  26.7 3.4 fusion.44
  30.9 4.1 copy.170
  35.7 1.7 reshape.230
  37.4 1.7 fusion.88
  40.1 1.7 copy.197
  41.7 1.5 copy.228
  43.2 5.1 reduce-window.26
  48.3 1.6 slice.129
  50.9 4.2 copy.172
  55.8 161.7 %all_gather.13 = f32[64,2,16]{2,1,0:T(2,128)} all-gather(f32[1,2,16]{2,1,0:T(2,128)S(1)} %copy-done.16), channel_id=1, replica_groups=mesh['seq'=64,'head'=2] {'seq'}, dimensions={0}, use_global_device_ids=true | all-gather | bytes 8320 | tf_op jit(solution)/shard_map/all_gather | solution.py:13
  217.5 1.6 bitcast_bitcast_fusion
  219.3 1.2 fusion.92
  220.5 1.9 fusion.55
  223.5 8.1 %fusion.27 = f32[256,2,16,64]{0,3,2,1:T(8,128)} fusion(f32[2,16,64,256]{3,2,1,0:T(8,128)S(1)} %fusion.94, bf16[256,2,16,64]{0,3,2,1:T(8,128)(2,1)S(1)} %bitcast.162, f32[2,16,256]{2,1,0:T(8,128)S(1)} %bitcast.182, f32[2,16,256]{2,1,0:T(8,128)S(1)} %copy-done.9, f32[2,256,256]{2,1,0:T(8,128)S(1)} %fusion.93, pred[256,256]{1,0:T(8,128)(4,1)S(1)} %iota_compare_fusion, ...), kind=kOutput, calls=%fused_computation.36 | convolution fusion | flops 1622147072 | bytes 5931008 | tf_op jit(solution)/shard_map/gkts,sgkp->tgkp/dot_general | solution.py:39
  231.6 8.1 %fusion.28 = f32[256,2,16,64]{0,3,2,1:T(8,128)} fusion(f32[2,16,64,256]{3,2,1,0:T(8,128)S(1)} %fusion.55, bf16[256,2,16,64]{0,3,2,1:T(8,128)(2,1)S(1)} %bitcast.160, f32[2,16,256]{2,1,0:T(8,128)S(1)} %bitcast.180, f32[2,16,256]{2,1,0:T(8,128)S(1)} %copy-done.10, f32[2,256,256]{2,1,0:T(8,128)S(1)} %fusion.92, pred[256,256]{1,0:T(8,128)(4,1)S(1)} %iota_compare_fusion, ...), kind=kOutput, calls=%fused_computation.38 | convolution fusion | flops 1622147072 | bytes 5931008 | tf_op jit(solution)/shard_map/gkts,sgkp->tgkp/dot_general | solution.py:39
  239.7 70.7 %all-gather.6.cloned.1.call-done = f32[128,16,64,128]{3,2,1,0:T(8,128)} async-done(((f32[2,16,64,128]{3,2,1,0:T(8,128)}), f32[128,16,64,128]{3,2,1,0:T(8,128)}) %all-gather.6.cloned.1.call-update) | async-done | bytes 67108880 | tf_op jit(solution)/shard_map/all_gather | solution.py:13
  311.4 7.5 %multiply_reduce_fusion = (f32[512,2]{0,1:T(2,128)S(1)}, f32[512,2,16,64]{0,3,2,1:T(8,128)}) fusion(f32[512,2048]{0,1:T(8,128)} %copy.172, f32[512,2,16,64]{0,3,2,1:T(8,128)} %bitcast.156, f32[2,16]{1,0:T(2,128)S(1)} %mul.167, f32[2,16,64,128]{3,2,1,0:T(8,128)S(1)} %get-tuple-element.47, bf16[512,2,128,1]{2,1,0,3:T(2,128)(2,1)S(1)} %bitcast.171, ...), kind=kOutput, calls=%fused_computation.22 | convolution fusion | flops 1623194624 | bytes 18157696 | tf_op jit(solution)/shard_map/tgn,gkpn->tgkp/dot_general | solution.py:47
  319.1 1.1 mul.175
  320.3 4.0 copy.207
  324.3 5.6 copy.171
  329.9 209.9 %all-gather.4.cloned.1.call-done = bf16[2048,8192]{1,0:T(8,128)(2,1)} async-done(((bf16[2048,128]{1,0:T(8,128)(2,1)}), bf16[2048,8192]{1,0:T(8,128)(2,1)}) %all-gather.4.cloned.1.call-update) | async-done | bytes 33554448 | tf_op jit(solution)/shard_map/all_gather | solution.py:127
  539.8 29.4 %convolution_convert_fusion = bf16[512,8192]{1,0:T(8,128)(2,1)} fusion(bf16[2048,8192]{1,0:T(8,128)(2,1)} %all-gather.4.cloned.1.call-done, f32[512,2048]{1,0:T(8,128)} %bitcast.158, f32[512,2048]{1,0:T(8,128)} %copy.171, f32[2048]{0:T(1024)S(1)} %copy-done.19, bf16[512,2048]{1,0:T(8,128)(2,1)S(1)} %copy-done.2), kind=kOutput, calls=%fused_computation.2 | convolution fusion | flops 17193500672 | bytes 52436992 | tf_op jit(solution)/shard_map/dot_general | solution.py:125
  569.8 2.9 collective-permute-start
  572.8 1.9 collective-permute-start.1
  575.4 14.0 %reduce-scatter.2.cloned.1.call-done = bf16[512,4096]{1,0:T(8,128)(2,1)} async-done(((bf16[512,8192]{1,0:T(8,128)(2,1)}), bf16[512,4096]{1,0:T(8,128)(2,1)}) %reduce-scatter.2.cloned.1.call-update) | async-done | bytes 4194320 | tf_op jit(solution)/shard_map/reduce_scatter | solution.py:130
  589.4 3.1 fusion.58
  592.5 1.5 collective-permute-start.2
  595.3 11.2 %all-to-all-start.1 = ((s32[64,2,2]{1,2,0:T(2,128)}), s32[64,2,2]{1,2,0:T(2,128)S(1)}, u32[]{:S(2)}, u32[]{:S(2)}) async-start(s32[64,2,2]{1,2,0:T(2,128)} %copy.174), calls=%async_computation.2 | async-start | bytes 131072 | tf_op jit(solution)/shard_map/all_to_all | solution.py:164
  606.5 3.1 fusion.62
  609.6 9.9 %collective-permute-done.2 = f32[64,4096]{1,0:T(8,128)} collective-permute-done((f32[64,4096]{1,0:T(8,128)S(1)}, f32[64,4096]{1,0:T(8,128)}, u32[]{:S(2)}, u32[]{:S(2)}) %collective-permute-start.2) | collective-permute-done | bytes 1048608 | tf_op jit(solution)/shard_map/ppermute | solution.py:27
  619.5 2.3 fusion.50
  621.8 2.2 reshape.235
  624.4 13.6 %all-to-all-start = ((f32[64,2,4096]{2,1,0:T(2,128)}), f32[64,2,4096]{2,1,0:T(2,128)S(1)}, u32[]{:S(2)}, u32[]{:S(2)}) async-start(f32[64,2,4096]{2,1,0:T(2,128)} %reshape.235), calls=%async_computation.1 | async-start | bytes 4194304 | tf_op jit(solution)/shard_map/all_to_all | solution.py:163
  638.6 26.5 %all-to-all-done = f32[64,2,4096]{2,1,0:T(2,128)S(1)} async-done(((f32[64,2,4096]{2,1,0:T(2,128)}), f32[64,2,4096]{2,1,0:T(2,128)S(1)}, u32[]{:S(2)}, u32[]{:S(2)}) %all-to-all-start) | async-done | bytes 2097184 | tf_op jit(solution)/shard_map/all_to_all | solution.py:163
  665.2 2.1 divide_convert_fusion.1
  667.2 2.3 convert_element_type.56
  669.5 2.3 fusion.47
  672.1 2.5 reshape.236
  674.6 20.0 %all-reduce.2.cloned.1.call-done = f32[128,128]{1,0:T(8,128)} async-done(((f32[128,128]{1,0:T(8,128)}), f32[128,128]{1,0:T(8,128)}) %all-reduce.2.cloned.1.call-update) | async-done | bytes 65552 | tf_op jit(solution)/shard_map/psum | solution.py:173
  697.1 3.5 convolution_bitcast_fusion
  (112 shorter events, 19.8 us)
Async XLA Ops:
  7.2 662.3 %copy-start = (bf16[1,4096,128]{2,1,0:T(8,128)(2,1)S(1)}, bf16[1,4096,128]{2,1,0:T(8,128)(2,1)}, u32[]{:S(2)}) copy-start(bf16[1,4096,128]{2,1,0:T(8,128)(2,1)} %param.25) | copy-start | bytes 3145732
  7.2 303.2 %all-gather.6.cloned.1.call-start = ((), (), s32[]{:S(2)}) async-start(), calls=%async_computation.6 | async-start | bytes 68157440 | tf_op jit(solution)/shard_map/all_gather | solution.py:13
  9.3 5.1 copy-start.3
  9.5 0.7 copy-start.13
  11.3 3.0 copy-start.4
  11.5 2.8 copy-start.14
  14.3 0.5 copy-start.15
  30.1 509.7 %all-gather.4.cloned.1.call-start = ((), (), s32[]{:S(2)}) async-start(), calls=%async_computation.3 | async-start | bytes 34078720 | tf_op jit(solution)/shard_map/all_gather | solution.py:127
  30.9 558.5 %reduce-scatter.2.cloned.1.call-start = ((), (), s32[]{:S(2)}) async-start(), calls=%async_computation.4 | async-start | bytes 12582912 | tf_op jit(solution)/shard_map/reduce_scatter | solution.py:130
  35.7 20.1 %copy-start.16 = (f32[1,2,16]{2,1,0:T(2,128)S(1)}, f32[1,2,16]{2,1,0:T(2,128)}, u32[]{:S(2)}) copy-start(f32[1,2,16]{2,1,0:T(2,128)} %copy.167) | copy-start | bytes 388
  55.8 167.6 %copy-start.1 = (bf16[256,2048]{0,1:T(8,128)(2,1)S(1)}, bf16[256,2048]{0,1:T(8,128)(2,1)}, u32[]{:S(2)}) copy-start(bf16[256,2048]{0,1:T(8,128)(2,1)} %copy.160) | copy-start | bytes 3145732
  55.8 167.6 %copy-start.7 = (f32[256,32]{0,1:T(8,128)S(1)}, f32[256,32]{0,1:T(8,128)}, u32[]{:S(2)}) copy-start(f32[256,32]{0,1:T(8,128)} %get-tuple-element.84) | copy-start | bytes 98308
  55.8 167.6 %copy-start.9 = (f32[2,16,256]{2,1,0:T(8,128)S(1)}, f32[2,16,256]{2,1,0:T(8,128)}, u32[]{:S(2)}) copy-start(f32[2,16,256]{2,1,0:T(8,128)} %get-tuple-element.92) | copy-start | bytes 98308
  55.8 167.6 %copy-start.12 = (f32[256,2,16]{0,2,1:T(8,128)S(1)}, f32[256,2,16]{0,2,1:T(8,128)}, u32[]{:S(2)}) copy-start(f32[256,2,16]{0,2,1:T(8,128)} %get-tuple-element.87) | copy-start | bytes 98308
  223.4 8.2 %copy-start.6 = (f32[256,32]{0,1:T(8,128)S(1)}, f32[256,32]{0,1:T(8,128)}, u32[]{:S(2)}) copy-start(f32[256,32]{0,1:T(8,128)} %get-tuple-element.85) | copy-start | bytes 98308
  223.4 8.2 %copy-start.10 = (f32[2,16,256]{2,1,0:T(8,128)S(1)}, f32[2,16,256]{2,1,0:T(8,128)}, u32[]{:S(2)}) copy-start(f32[2,16,256]{2,1,0:T(8,128)} %get-tuple-element.95) | copy-start | bytes 98308
  223.5 8.1 %copy-start.11 = (f32[256,2,16]{0,2,1:T(8,128)S(1)}, f32[256,2,16]{0,2,1:T(8,128)}, u32[]{:S(2)}) copy-start(f32[256,2,16]{0,2,1:T(8,128)} %get-tuple-element.100) | copy-start | bytes 98308
  310.5 1.0 copy-start.5
  310.5 0.9 copy-start.8
  324.3 215.5 %copy-start.2 = (bf16[512,2048]{1,0:T(8,128)(2,1)S(1)}, bf16[512,2048]{1,0:T(8,128)(2,1)}, u32[]{:S(2)}) copy-start(bf16[512,2048]{1,0:T(8,128)(2,1)} %param.17) | copy-start | bytes 6291460
  324.3 215.5 %copy-start.19 = (f32[2048]{0:T(1024)S(1)}, f32[2048]{0:T(1024)}, u32[]{:S(2)}) copy-start(f32[2048]{0:T(1024)} %param.23) | copy-start | bytes 24580
  569.2 0.7 copy-start.18
  569.2 3.6 copy-start.17
  569.2 5.5 copy-start.20
  569.8 24.1 %copy-start.21 = (s32[64,1]{0,1:T(1,128)S(1)}, s32[64,1]{0,1:T(1,128)}, u32[]{:S(2)}) copy-start(s32[64,1]{0,1:T(1,128)} %param.28) | copy-start | bytes 772
  569.8 4.9 collective-permute-start
  572.8 2.6 collective-permute-start.1
  592.5 27.0 %collective-permute-start.2 = (f32[64,4096]{1,0:T(8,128)S(1)}, f32[64,4096]{1,0:T(8,128)}, u32[]{:S(2)}, u32[]{:S(2)}) collective-permute-start(f32[64,4096]{1,0:T(8,128)S(1)} %fusion.58), channel_id=1, source_target_pairs={{2,0},{4,2},{6,4},{8,6},{10,8},{12,10},{14,12},{16,14},{18,16},{20... | collective-permute-start | bytes 3145736 | tf_op jit(solution)/shard_map/ppermute | solution.py:27
  595.3 29.2 %all-to-all-start.1 = ((s32[64,2,2]{1,2,0:T(2,128)}), s32[64,2,2]{1,2,0:T(2,128)S(1)}, u32[]{:S(2)}, u32[]{:S(2)}) async-start(s32[64,2,2]{1,2,0:T(2,128)} %copy.174), calls=%async_computation.2 | async-start | bytes 131072 | tf_op jit(solution)/shard_map/all_to_all | solution.py:164
  624.4 40.7 %all-to-all-start = ((f32[64,2,4096]{2,1,0:T(2,128)}), f32[64,2,4096]{2,1,0:T(2,128)S(1)}, u32[]{:S(2)}, u32[]{:S(2)}) async-start(f32[64,2,4096]{2,1,0:T(2,128)} %reshape.235), calls=%async_computation.1 | async-start | bytes 4194304 | tf_op jit(solution)/shard_map/all_to_all | solution.py:163
  638.0 56.6 %all-reduce.2.cloned.1.call-start = ((), (), s32[]{:S(2)}) async-start(), calls=%async_computation.5 | async-start | bytes 131072 | tf_op jit(solution)/shard_map/psum | solution.py:173
Sparse Core Ops, SparseCore 0:
  30.2 280.0 all-gather.5
  313.0 226.7 all-gather.3
  569.3 19.9 reduce-scatter.1
  671.9 22.6 all-reduce.1
where the time goes:
time: 712 us; the launch traced here: 707 us
  waiting for transfers between devices  353 us (50%)
  blocking collectives  162 us (23%)
  matrix products  76.9 us (11%)
  local copies, waits for them, and re-layouts  51.5 us (7%)
  starting transfers between devices  31.3 us (4%)
  other arithmetic  18.6 us (3%)
  between operations  14.2 us (2%)
    all_gather x1, waiting for transfers between devices, on_device(): lax.all_gather(out_weight, 'seq', axis=1, tiled=True)  210 us
    all_gather x1, blocking collectives, prefix(): gathered = jax.tree.map(lambda a: lax.all_gather(a, axis), part)  162 us
    all_gather x1, waiting for transfers between devices, prefix(): gathered = jax.tree.map(lambda a: lax.all_gather(a, axis), part)  70.7 us
    dot_general x1, matrix products, on_device(): jnp.dot(y_out, lax.all_gather(out_weight, 'seq', axis=1, tiled=True), pre...  29.4 us
    all_to_all x1, waiting for transfers between devices, on_device(): lax.all_to_all(send_sums, 'seq', split_axis=0, concat_axis=0, tiled=True)  26.5 us
    psum x1, waiting for transfers between devices, on_device(): logits = lax.psum(partial_logits, 'head')  20 us
    dot_general x2, matrix products, segment_summands(): intra = jnp.einsum('gkts,sgkp->tgkp', weights, xs, precision=high)  16.2 us
  transfers between devices with their start and end apart: 9, of which 8 were waited for; matrix products, arithmetic and copies ran while one was open for 11% of the time, Pallas kernels for 0%

commit v1 on v0

--- a/solution.py
+++ b/solution.py
@@ -6,19 +6,6 @@
 HEAD_DIM = 64
 STATE = 128
 CAP = 2
-
-
-def prefix(part, axis, combine, identity):
-    place = lax.axis_index(axis)
-    gathered = jax.tree.map(lambda a: lax.all_gather(a, axis), part)
-    state = jax.tree.map(lambda a, e: jnp.zeros_like(a) + jnp.asarray(e, a.dtype), part, identity)
-
-    def one(step, state):
-        return combine(
-            state, jax.tree.map(lambda a: lax.dynamic_index_in_dim(a, step, 0, False), gathered)
-        )
-
-    return lax.fori_loop(0, place, one, state)
 
 
 def from_behind(value, axis, steps):
@@ -70,6 +57,21 @@
         total = total + piece_total
     return (jnp.concatenate(results, axis=0), state, total)
 
+
+def exclusive_scan(part, axis):
+    count = lax.axis_size(axis)
+    place = lax.axis_index(axis)
+    inclusive = part
+    exclusive = None
+    step = 1
+    while step < count:
+        pairs = [(source, source + step) for source in range(count - step)]
+        got = jax.tree.map(lambda a: lax.ppermute(a, axis, pairs), inclusive)
+        exclusive = got if exclusive is None else combine_states(got, exclusive)
+        if step * 2 < count:
+            inclusive = combine_states(got, inclusive)
+        step *= 2
+    return exclusive[0]
 
 def combine_states(earlier, later):
     return (earlier[0] * jnp.exp(later[1])[..., None, None] + later[0], earlier[1] + later[1])
@@ -108,8 +110,7 @@
     logd = log_decay.reshape(tok, groups_here, per_group)
     cum = jnp.cumsum(logd, axis=0)
     intra, local_state, total = piecewise_terms(xs, bmat, cmat, dtk, logd)
-    identity = (jnp.zeros_like(local_state), jnp.zeros_like(total))
-    state_in, unused = prefix((local_state, total), "seq", combine_states, identity)
+    state_in = exclusive_scan((local_state, total), "seq")
     ssm = (
         intra
         + inter_term(cmat, cum, state_in)
@@ -131,18 +132,14 @@
         partial_out.astype(jnp.bfloat16), "head", scatter_dimension=1, tiled=True
     )
     base = lax.axis_index("seq") * tok
-    prev_start, prev_len = from_behind((span_start, span_len), "seq", 1)
-    place = base + jnp.arange(tok, dtype=jnp.int32)
-    spill_sums = jnp.dot(
-        inside_mask(prev_start, prev_len, place), layer_out, preferred_element_type=jnp.float32
-    )
-    returned = from_behind(spill_sums, "seq", -1)
-    sums = (
-        jnp.dot(
-            inside_mask(span_start, span_len, place), layer_out, preferred_element_type=jnp.float32
-        )
-        + returned
-    )
+    reach = min(tok, 128)
+    following = from_behind(layer_out[:reach], "seq", -1)
+    rows = jnp.concatenate([layer_out, following], axis=0)
+    place = base + jnp.arange(tok + reach, dtype=jnp.int32)
+    sums = jnp.dot(
+        inside_mask(span_start, span_len, place), rows, preferred_element_type=jnp.float32
+    )
+    own_feature = (sums / span_len[:, None].astype(jnp.float32)).astype(jnp.bfloat16)
     count = span_start.shape[0]
     owners = lax.axis_size("seq")
     slots_total = owners * CAP
@@ -153,24 +150,21 @@
     slot = jnp.sum(jnp.logical_and(same, earlier), axis=1)
     target_labels = owner * CAP + slot
     pick = jnp.arange(slots_total, dtype=jnp.int32)[:, None] == target_labels[None, :]
-    send_sums = jnp.dot(pick.astype(jnp.float32), sums, precision=lax.Precision.HIGHEST).reshape(
-        owners, CAP, -1
-    )
-    label_slots = jnp.sum(jnp.where(pick, span_label[None, :] + 1, 0), axis=1) - 1
-    length_slots = jnp.sum(jnp.where(pick, span_len[None, :], 0), axis=1)
-    meta = jnp.stack([label_slots, length_slots], axis=-1).reshape(owners, CAP, 2)
-    got_sums, got_meta = (
-        lax.all_to_all(send_sums, "seq", split_axis=0, concat_axis=0, tiled=True),
-        lax.all_to_all(meta, "seq", split_axis=0, concat_axis=0, tiled=True),
-    )
-    labels = got_meta[:, :, 0].reshape(-1)
-    lengths = got_meta[:, :, 1].reshape(-1)
+    label_col = jnp.zeros((count, 128), jnp.bfloat16).at[:, 0].set(
+        span_label.astype(jnp.bfloat16)
+    )
+    packed = jnp.concatenate([own_feature, label_col], axis=1)
+    width = own_feature.shape[1]
+    empty = jnp.zeros((1, packed.shape[1]), jnp.bfloat16).at[0, width].set(-1.0)
+    chosen = jnp.where(jnp.any(pick, axis=1), jnp.argmax(pick, axis=1), count)
+    send = jnp.concatenate([packed, empty], axis=0)[chosen].reshape(owners, CAP, -1)
+    got = lax.all_to_all(send, "seq", split_axis=0, concat_axis=0, tiled=True)
+    got = got.reshape(slots_total, -1)
+    feature = got[:, :width]
+    labels = got[:, width].astype(jnp.int32)
     valid = labels >= 0
-    feature = (
-        got_sums.reshape(slots_total, -1) / jnp.maximum(lengths, 1)[:, None].astype(jnp.float32)
-    ).astype(jnp.bfloat16)
     partial_logits = jnp.dot(feature, probe[0], preferred_element_type=jnp.float32)
-    logits = lax.psum(partial_logits, "head")
+    logits = partial_logits + lax.ppermute(partial_logits, "head", [(0, 1), (1, 0)])
     top = jnp.max(logits, axis=1, keepdims=True)
     lse = top[:, 0] + jnp.log(jnp.sum(jnp.exp(logits - top), axis=1))
     onehot = jnp.arange(logits.shape[1])[None, :] == labels[:, None]

time: 712 us -> 455 us (0.64)
  waiting for transfers between devices: 353 us -> 194 us
  blocking collectives: 162 us -> 30.8 us
  starting transfers between devices: 31.3 us -> 68.6 us
  local copies, waits for them, and re-layouts: 51.5 us -> 43.2 us
  other arithmetic: 18.6 us -> 26.8 us
    all_gather x1 -> x0, blocking collectives: 162 us -> none  [prefix(): gathered = jax.tree.map(lambda a: lax.all_gather(a, axis), part)]
    all_gather x1, waiting for transfers between devices: 210 us -> 91.6 us  [on_device(): lax.all_gather(out_weight, 'seq', axis=1, tiled=True)]
    all_gather x1 -> x0, waiting for transfers between devices: 70.7 us -> none  [prefix(): gathered = jax.tree.map(lambda a: lax.all_gather(a, axis), part)]
    ppermute x0 -> x12, starting transfers between devices: none -> 67.3 us  [the longest x11 64.2 us: exclusive_scan(): got = jax.tree.map(lambda a: lax.ppermute(a, axis, pairs), inclusive)]
    ppermute x0 -> x12, waiting for transfers between devices: none -> 62.3 us  [the longest x11 61.5 us: exclusive_scan(): got = jax.tree.map(lambda a: lax.ppermute(a, axis, pairs), inclusive)]
    all_to_all x0 -> x1, blocking collectives: none -> 30.8 us  [on_device(): got = lax.all_to_all(send, 'seq', split_axis=0, concat_axis=0, tiled=True)]
    all_to_all x2 -> x0, waiting for transfers between devices: 26.9 us -> none  [the longest x1 26.5 us: on_device(): lax.all_to_all(send_sums, 'seq', split_axis=0, concat_axis=0, tiled=True)]
    all_to_all x2 -> x0, starting transfers between devices: 24.8 us -> none  [the longest x1 13.6 us: on_device(): lax.all_to_all(send_sums, 'seq', split_axis=0, concat_axis=0, tiled=True)]
  transfers between devices with their start and end apart: 9 -> 15, of which waited for: 8 -> 9; matrix products, arithmetic and copies ran while one was open for 11% -> 23% of each run, Pallas kernels for 0% -> 0%
where the time goes in v1:
time: 455 us; the launch traced here: 454 us
  waiting for transfers between devices  194 us (43%)
  matrix products  74.5 us (16%)
  starting transfers between devices  68.6 us (15%)
  local copies, waits for them, and re-layouts  43.2 us (9%)
  blocking collectives  30.8 us (7%)
  other arithmetic  26.8 us (6%)
  between operations  15.2 us (3%)
    all_gather x1, waiting for transfers between devices, on_device(): lax.all_gather(out_weight, 'seq', axis=1, tiled=True)  91.6 us
    ppermute x11, starting transfers between devices, exclusive_scan(): got = jax.tree.map(lambda a: lax.ppermute(a, axis, pairs), inclusive)  64.2 us
    ppermute x11, waiting for transfers between devices, exclusive_scan(): got = jax.tree.map(lambda a: lax.ppermute(a, axis, pairs), inclusive)  61.5 us
    all_to_all x1, blocking collectives, on_device(): got = lax.all_to_all(send, 'seq', split_axis=0, concat_axis=0, tiled=True)  30.8 us
    dot_general x1, matrix products, on_device(): jnp.dot(y_out, lax.all_gather(out_weight, 'seq', axis=1, tiled=True), pre...  29.3 us
    ppermute x1, waiting for transfers between devices, from_behind(): lax.ppermute(value, axis, [(source, source + steps) for source in range(l...  21.2 us
    dot_general x2, matrix products, segment_summands(): intra = jnp.einsum('gkts,sgkp->tgkp', weights, xs, precision=high)  19.6 us
    reduce_scatter x1, waiting for transfers between devices, on_device(): lax.psum_scatter(partial_out.astype(jnp.bfloat16), 'head', scatter_dimens...  18.7 us
  transfers between devices with their start and end apart: 15, of which 9 were waited for; matrix products, arithmetic and copies ran while one was open for 23% of the time, Pallas kernels for 0%

profile of v1, /device:TPU:1, one launch (start us, length us, event | category | flops | bytes accessed | tf_op | source)
XLA Modules:
  0.0 453.7 jit_solution(17357633671480904244)
XLA Ops:
  11.5 2.7 fusion.115
  14.3 1.5 copy.139
  15.8 1.6 fusion.117
  17.5 1.3 copy.149
  24.0 2.6 fusion.54
  26.6 4.4 collective-permute-start
  30.9 21.7 %collective-permute-done = f32[2,16,64,128]{3,2,1,0:T(8,128)S(1)} collective-permute-done((f32[2,16,64,128]{3,2,1,0:T(8,128)S(1)}, f32[2,16,64,128]{3,2,1,0:T(8,128)S(1)}, u32[]{:S(2)}, u32[]{:S(2)}) %collective-permute-start) | collective-permute-done | bytes 1048608 | tf_op jit(solution)/shard_map/ppermute | solution.py:69
  52.9 6.1 %collective-permute-start.1 = (f32[2,16,64,128]{3,2,1,0:T(8,128)S(1)}, f32[2,16,64,128]{3,2,1,0:T(8,128)S(1)}, u32[]{:S(2)}, u32[]{:S(2)}) collective-permute-start(f32[2,16,64,128]{3,2,1,0:T(8,128)S(1)} %multiply_add_fusion.4), channel_id=1, source_target_pairs={{0,4},{2,6},{4,8},{6,10},{8,12},{10,14},{12,16},{14,18},{16,20},{1... | collective-permute-start | bytes 3145736 | tf_op jit(solution)/shard_map/ppermute | solution.py:69
  59.0 6.3 %collective-permute-start.2 = (f32[2,16]{1,0:T(2,128)S(1)}, f32[2,16]{1,0:T(2,128)S(1)}, u32[]{:S(2)}, u32[]{:S(2)}) collective-permute-start(f32[2,16]{1,0:T(2,128)S(1)} %get-tuple-element.46), channel_id=1, source_target_pairs={{0,2},{2,4},{4,6},{6,8},{8,10},{10,12},{12,14},{14,16},{16,18},{18... | collective-permute-start | bytes 392 | tf_op jit(solution)/shard_map/ppermute | solution.py:69
  65.3 27.7 %collective-permute-done.2 = f32[2,16]{1,0:T(2,128)S(1)} collective-permute-done((f32[2,16]{1,0:T(2,128)S(1)}, f32[2,16]{1,0:T(2,128)S(1)}, u32[]{:S(2)}, u32[]{:S(2)}) %collective-permute-start.2) | collective-permute-done | bytes 160 | tf_op jit(solution)/shard_map/ppermute | solution.py:69
  94.8 7.2 %collective-permute-start.3 = (f32[2,16,64,128]{3,2,1,0:T(8,128)}, f32[2,16,64,128]{3,2,1,0:T(8,128)}, u32[]{:S(2)}, u32[]{:S(2)}) collective-permute-start(f32[2,16,64,128]{3,2,1,0:T(8,128)} %multiply_add_fusion.3), channel_id=1, source_target_pairs={{0,8},{2,10},{4,12},{6,14},{8,16},{10,18},{12,20},{14,22},{16,24},... | collective-permute-start | bytes 3145736 | tf_op jit(solution)/shard_map/ppermute | solution.py:69
  103.7 1.5 copy.213
  105.2 5.1 %reduce-window.26 = f32[16,2,4,128]{3,0,1,2:T(8,128)} reduce-window(f32[16,2,4,128]{3,0,1,2:T(8,128)} %bitcast.165, f32[]{:T(128)} %constant.85.clone.1), window={size=1x1x1x128 pad=0_0x0_0x0_0x127_0}, to_apply=%region_4.5 | reduce-window | flops 2080768 | bytes 131076 | tf_op jit(solution)/shard_map/reduce-window.4
  110.3 1.5 slice.170
  112.8 1.6 bitcast_bitcast_fusion
  115.5 5.0 %collective-permute-start.4 = (f32[2,16]{1,0:T(2,128)}, f32[2,16]{1,0:T(2,128)S(1)}, u32[]{:S(2)}, u32[]{:S(2)}) collective-permute-start(f32[2,16]{1,0:T(2,128)} %get-tuple-element.44), channel_id=1, source_target_pairs={{0,4},{2,6},{4,8},{6,10},{8,12},{10,14},{12,16},{14,18},{16,20},{1... | collective-permute-start | bytes 392 | tf_op jit(solution)/shard_map/ppermute | solution.py:69
  122.2 2.7 multiply_add_fusion.2
  124.8 10.2 %collective-permute-start.5 = (f32[2,16,64,128]{3,2,1,0:T(8,128)}, f32[2,16,64,128]{3,2,1,0:T(8,128)}, u32[]{:S(2)}, u32[]{:S(2)}) collective-permute-start(f32[2,16,64,128]{3,2,1,0:T(8,128)} %multiply_add_fusion.2), channel_id=1, source_target_pairs={{0,16},{2,18},{4,20},{6,22},{8,24},{10,26},{12,28},{14,30},{16,32}... | collective-permute-start | bytes 3145736 | tf_op jit(solution)/shard_map/ppermute | solution.py:69
  136.1 2.3 fusion.84
  138.4 2.3 fusion.123
  140.7 2.7 collective-permute-start.6
  143.4 4.2 copy.158
  148.3 6.0 %collective-permute-done.6 = f32[2,16]{1,0:T(2,128)S(1)} collective-permute-done((f32[2,16]{1,0:T(2,128)S(1)}, f32[2,16]{1,0:T(2,128)S(1)}, u32[]{:S(2)}, u32[]{:S(2)}) %collective-permute-start.6) | collective-permute-done | bytes 160 | tf_op jit(solution)/shard_map/ppermute | solution.py:69
  154.3 2.7 multiply_add_fusion.1
  157.0 10.9 %collective-permute-start.7 = (f32[2,16,64,128]{3,2,1,0:T(8,128)}, f32[2,16,64,128]{3,2,1,0:T(8,128)}, u32[]{:S(2)}, u32[]{:S(2)}) collective-permute-start(f32[2,16,64,128]{3,2,1,0:T(8,128)} %multiply_add_fusion.1), channel_id=1, source_target_pairs={{0,32},{2,34},{4,36},{6,38},{8,40},{10,42},{12,44},{14,46},{16,48}... | collective-permute-start | bytes 3145736 | tf_op jit(solution)/shard_map/ppermute | solution.py:69
  167.9 9.7 %fusion.37 = f32[256,2,16,64]{0,3,2,1:T(8,128)} fusion(f32[2,16,64,256]{3,2,1,0:T(8,128)} %fusion.123, bf16[256,2,16,64]{0,3,2,1:T(8,128)(2,1)S(1)} %bitcast.154, f32[2,16,256]{2,1,0:T(8,128)S(1)} %bitcast.173, f32[2,16,256]{2,1,0:T(8,128)S(1)} %copy-done.17, f32[2,256,256]{2,1,0:T(8,128)} %fusion.122, pred[256,256]{1,0:T(8,128)(4,1)S(1)} %iota_compare_fusion.2, ...), kind=kOutput, calls=%fused_computation.41 | convolution fusion | flops 1622147072 | bytes 5931008 | tf_op jit(solution)/shard_map/gkts,sgkp->tgkp/dot_general | solution.py:26
  177.6 1.4 collective-permute-start.8
  179.0 4.1 copy.160
  183.7 2.6 collective-permute-done.7
  186.3 2.8 multiply_add_fusion
  189.1 6.7 %collective-permute-start.9 = (f32[2,16,64,128]{3,2,1,0:T(8,128)}, f32[2,16,64,128]{3,2,1,0:T(8,128)}, u32[]{:S(2)}, u32[]{:S(2)}) collective-permute-start(f32[2,16,64,128]{3,2,1,0:T(8,128)} %multiply_add_fusion), channel_id=1, source_target_pairs={{0,64},{2,66},{4,68},{6,70},{8,72},{10,74},{12,76},{14,78},{16,80}... | collective-permute-start | bytes 3145736 | tf_op jit(solution)/shard_map/ppermute | solution.py:69
  195.7 9.9 %fusion.38 = f32[256,2,16,64]{0,3,2,1:T(8,128)} fusion(f32[2,16,64,256]{3,2,1,0:T(8,128)} %fusion.84, bf16[256,2,16,64]{0,3,2,1:T(8,128)(2,1)S(1)} %bitcast.152, f32[2,16,256]{2,1,0:T(8,128)S(1)} %bitcast.171, f32[2,16,256]{2,1,0:T(8,128)S(1)} %copy-done.16, f32[2,256,256]{2,1,0:T(8,128)} %fusion.121, pred[256,256]{1,0:T(8,128)(4,1)} %copy-done.15, ...), kind=kOutput, calls=%fused_computation.43 | convolution fusion | flops 1622147072 | bytes 5931008 | tf_op jit(solution)/shard_map/gkts,sgkp->tgkp/dot_general | solution.py:26
  205.7 3.5 collective-permute-start.10
  209.9 3.4 collective-permute-done.10
  213.4 9.2 %multiply_reduce_fusion = (f32[512,2]{0,1:T(2,128)S(1)}, f32[512,2,16,64]{0,3,2,1:T(8,128)}) fusion(f32[512,2048]{0,1:T(8,128)} %copy.160, f32[512,2,16,64]{0,3,2,1:T(8,128)} %bitcast.148, f32[2,16]{1,0:T(2,128)S(1)} %mul.255, bf16[512,2,128,1]{2,1,0,3:T(2,128)(2,1)S(1)} %bitcast.163, f32[2,16,64,128]{3,2,1,0:T(8,128)S(1)} %copy-done.4, ...), kind=kOutput, calls=%fused_computation.27 | convolution fusion | flops 1625816064 | bytes 23401216 | tf_op jit(solution)/shard_map/tgn,gkpn->tgkp/dot_general | solution.py:34
  223.9 4.0 copy.192
  227.8 5.5 %copy.159 = f32[512,2048]{1,0:T(8,128)} copy(f32[512,2048]{0,1:T(8,128)} %bitcast.149) | data formatting | bytes 8388608 | tf_op jit(solution)/shard_map/reshape | solution.py:119
  233.4 91.6 %all-gather.2.cloned.1.call-done = bf16[2048,8192]{1,0:T(8,128)(2,1)} async-done(((bf16[2048,128]{1,0:T(8,128)(2,1)}), bf16[2048,8192]{1,0:T(8,128)(2,1)}) %all-gather.2.cloned.1.call-update) | async-done | bytes 33554448 | tf_op jit(solution)/shard_map/all_gather | solution.py:128
  325.0 29.3 %convolution_convert_fusion = bf16[512,8192]{1,0:T(8,128)(2,1)} fusion(bf16[2048,8192]{1,0:T(8,128)(2,1)} %all-gather.2.cloned.1.call-done, f32[512,2048]{1,0:T(8,128)} %bitcast.150, f32[512,2048]{1,0:T(8,128)} %copy.159, f32[2048]{0:T(1024)S(1)} %copy-done.21, bf16[512,2048]{1,0:T(8,128)(2,1)S(1)} %copy-done.2), kind=kOutput, calls=%fused_computation.1 | convolution fusion | flops 17193500672 | bytes 52436992 | tf_op jit(solution)/shard_map/dot_general | solution.py:126
  355.9 18.7 %reduce-scatter.2.cloned.1.call-done = bf16[512,4096]{1,0:T(8,128)(2,1)} async-done(((bf16[512,8192]{1,0:T(8,128)(2,1)}), bf16[512,4096]{1,0:T(8,128)(2,1)}) %reduce-scatter.2.cloned.1.call-update) | async-done | bytes 4194320 | tf_op jit(solution)/shard_map/reduce_scatter | solution.py:131
  374.5 1.3 slice.173
  380.9 21.2 %collective-permute-done.11 = bf16[128,4096]{1,0:T(8,128)(2,1)} collective-permute-done((bf16[128,4096]{1,0:T(8,128)(2,1)S(1)}, bf16[128,4096]{1,0:T(8,128)(2,1)}, u32[]{:S(2)}, u32[]{:S(2)}) %collective-permute-start.11) | collective-permute-done | bytes 1048608 | tf_op jit(solution)/shard_map/ppermute | solution.py:14
  402.2 3.6 fusion.21
  405.8 1.3 gather_fusion
  407.6 30.8 %all_to_all.5 = bf16[64,2,4224]{2,1,0:T(2,128)(2,1)} all-to-all(bf16[64,2,4224]{2,1,0:T(2,128)(2,1)S(1)} %reshape.274), channel_id=1, replica_groups=mesh['seq'=64,'head'=2] {'seq'}, dimensions={0} | all-to-all | bytes 2162688 | tf_op jit(solution)/shard_map/all_to_all | solution.py:161
  438.4 1.5 reshape.275
  440.6 3.0 collective-permute-start.12
  445.1 1.8 convolution_bitcast_fusion
  (132 shorter events, 30.0 us)
Async XLA Ops:
  7.2 432.9 %copy-start = (bf16[1,4096,128]{2,1,0:T(8,128)(2,1)S(1)}, bf16[1,4096,128]{2,1,0:T(8,128)(2,1)}, u32[]{:S(2)}) copy-start(bf16[1,4096,128]{2,1,0:T(8,128)(2,1)} %param.27) | copy-start | bytes 3145732
  7.2 317.8 %all-gather.2.cloned.1.call-start = ((), (), s32[]{:S(2)}) async-start(), calls=%async_computation.2 | async-start | bytes 34078720 | tf_op jit(solution)/shard_map/all_gather | solution.py:128
  7.9 366.6 %reduce-scatter.2.cloned.1.call-start = ((), (), s32[]{:S(2)}) async-start(), calls=%async_computation.3 | async-start | bytes 12582912 | tf_op jit(solution)/shard_map/reduce_scatter | solution.py:131
  11.5 9.8 %copy-start.13 = (f32[512,32]{0,1:T(8,128)S(1)}, f32[512,32]{0,1:T(8,128)}, u32[]{:S(2)}) copy-start(f32[512,32]{0,1:T(8,128)} %param.22) | copy-start | bytes 196612
  21.4 1.4 copy-start.9
  21.4 2.6 copy-start.11
  24.0 78.0 %copy-start.6 = (bf16[512,256]{1,0:T(8,128)(2,1)S(1)}, bf16[512,256]{1,0:T(8,128)(2,1)}, u32[]{:S(2)}) copy-start(bf16[512,256]{1,0:T(8,128)(2,1)} %param.21) | copy-start | bytes 786436
  26.6 26.1 %collective-permute-start = (f32[2,16,64,128]{3,2,1,0:T(8,128)S(1)}, f32[2,16,64,128]{3,2,1,0:T(8,128)S(1)}, u32[]{:S(2)}, u32[]{:S(2)}) collective-permute-start(f32[2,16,64,128]{3,2,1,0:T(8,128)S(1)} %fusion.54), channel_id=1, source_target_pairs={{0,2},{2,4},{4,6},{6,8},{8,10},{10,12},{12,14},{14,16},{16,18},{18... | collective-permute-start | bytes 3145736 | tf_op jit(solution)/shard_map/ppermute | solution.py:69
  52.7 50.0 %copy-start.3 = (f32[2,16,64,128]{3,2,1,0:T(8,128)}, f32[2,16,64,128]{3,2,1,0:T(8,128)S(1)}, u32[]{:S(2)}) copy-start(f32[2,16,64,128]{3,2,1,0:T(8,128)S(1)} %collective-permute-done) | copy-start | bytes 3145732
  52.9 40.7 %collective-permute-start.1 = (f32[2,16,64,128]{3,2,1,0:T(8,128)S(1)}, f32[2,16,64,128]{3,2,1,0:T(8,128)S(1)}, u32[]{:S(2)}, u32[]{:S(2)}) collective-permute-start(f32[2,16,64,128]{3,2,1,0:T(8,128)S(1)} %multiply_add_fusion.4), channel_id=1, source_target_pairs={{0,4},{2,6},{4,8},{6,10},{8,12},{10,14},{12,16},{14,18},{16,20},{1... | collective-permute-start | bytes 3145736 | tf_op jit(solution)/shard_map/ppermute | solution.py:69
  59.0 34.0 %collective-permute-start.2 = (f32[2,16]{1,0:T(2,128)S(1)}, f32[2,16]{1,0:T(2,128)S(1)}, u32[]{:S(2)}, u32[]{:S(2)}) collective-permute-start(f32[2,16]{1,0:T(2,128)S(1)} %get-tuple-element.46), channel_id=1, source_target_pairs={{0,2},{2,4},{4,6},{6,8},{8,10},{10,12},{12,14},{14,16},{16,18},{18... | collective-permute-start | bytes 392 | tf_op jit(solution)/shard_map/ppermute | solution.py:69
  93.6 9.2 %copy-start.5 = (f32[2,16,64,128]{3,2,1,0:T(8,128)}, f32[2,16,64,128]{3,2,1,0:T(8,128)S(1)}, u32[]{:S(2)}) copy-start(f32[2,16,64,128]{3,2,1,0:T(8,128)S(1)} %collective-permute-done.1) | copy-start | bytes 3145732
  94.8 27.3 %collective-permute-start.3 = (f32[2,16,64,128]{3,2,1,0:T(8,128)}, f32[2,16,64,128]{3,2,1,0:T(8,128)}, u32[]{:S(2)}, u32[]{:S(2)}) collective-permute-start(f32[2,16,64,128]{3,2,1,0:T(8,128)} %multiply_add_fusion.3), channel_id=1, source_target_pairs={{0,8},{2,10},{4,12},{6,14},{8,16},{10,18},{12,20},{14,22},{16,24},... | collective-permute-start | bytes 3145736 | tf_op jit(solution)/shard_map/ppermute | solution.py:69
  115.5 6.1 %collective-permute-start.4 = (f32[2,16]{1,0:T(2,128)}, f32[2,16]{1,0:T(2,128)S(1)}, u32[]{:S(2)}, u32[]{:S(2)}) collective-permute-start(f32[2,16]{1,0:T(2,128)} %get-tuple-element.44), channel_id=1, source_target_pairs={{0,4},{2,6},{4,8},{6,10},{8,12},{10,14},{12,16},{14,18},{16,20},{1... | collective-permute-start | bytes 392 | tf_op jit(solution)/shard_map/ppermute | solution.py:69
  124.8 29.5 %collective-permute-start.5 = (f32[2,16,64,128]{3,2,1,0:T(8,128)}, f32[2,16,64,128]{3,2,1,0:T(8,128)}, u32[]{:S(2)}, u32[]{:S(2)}) collective-permute-start(f32[2,16,64,128]{3,2,1,0:T(8,128)} %multiply_add_fusion.2), channel_id=1, source_target_pairs={{0,16},{2,18},{4,20},{6,22},{8,24},{10,26},{12,28},{14,30},{16,32}... | collective-permute-start | bytes 3145736 | tf_op jit(solution)/shard_map/ppermute | solution.py:69
  138.4 9.2 %copy-start.7 = (bf16[512,256]{1,0:T(8,128)(2,1)S(1)}, bf16[512,256]{1,0:T(8,128)(2,1)}, u32[]{:S(2)}) copy-start(bf16[512,256]{1,0:T(8,128)(2,1)} %param.21) | copy-start | bytes 786436
  140.7 27.2 %copy-start.1 = (bf16[256,2048]{0,1:T(8,128)(2,1)S(1)}, bf16[256,2048]{0,1:T(8,128)(2,1)}, u32[]{:S(2)}) copy-start(bf16[256,2048]{0,1:T(8,128)(2,1)} %copy.149) | copy-start | bytes 3145732
  140.7 27.2 %copy-start.12 = (f32[256,32]{0,1:T(8,128)S(1)}, f32[256,32]{0,1:T(8,128)}, u32[]{:S(2)}) copy-start(f32[256,32]{0,1:T(8,128)} %copy-done.11) | copy-start | bytes 98308
  140.7 27.2 %copy-start.17 = (f32[2,16,256]{2,1,0:T(8,128)S(1)}, f32[2,16,256]{2,1,0:T(8,128)}, u32[]{:S(2)}) copy-start(f32[2,16,256]{2,1,0:T(8,128)} %get-tuple-element.60) | copy-start | bytes 98308
  140.7 27.2 %copy-start.18 = (f32[256,2,16]{0,2,1:T(8,128)S(1)}, f32[256,2,16]{0,2,1:T(8,128)}, u32[]{:S(2)}) copy-start(f32[256,2,16]{0,2,1:T(8,128)} %get-tuple-element.58) | copy-start | bytes 98308
  140.7 13.6 %collective-permute-start.6 = (f32[2,16]{1,0:T(2,128)S(1)}, f32[2,16]{1,0:T(2,128)S(1)}, u32[]{:S(2)}, u32[]{:S(2)}) collective-permute-start(f32[2,16]{1,0:T(2,128)S(1)} %get-tuple-element.42), channel_id=1, source_target_pairs={{0,8},{2,10},{4,12},{6,14},{8,16},{10,18},{12,20},{14,22},{16,24},... | collective-permute-start | bytes 392 | tf_op jit(solution)/shard_map/ppermute | solution.py:69
  157.0 29.3 %collective-permute-start.7 = (f32[2,16,64,128]{3,2,1,0:T(8,128)}, f32[2,16,64,128]{3,2,1,0:T(8,128)}, u32[]{:S(2)}, u32[]{:S(2)}) collective-permute-start(f32[2,16,64,128]{3,2,1,0:T(8,128)} %multiply_add_fusion.1), channel_id=1, source_target_pairs={{0,32},{2,34},{4,36},{6,38},{8,40},{10,42},{12,44},{14,46},{16,48}... | collective-permute-start | bytes 3145736 | tf_op jit(solution)/shard_map/ppermute | solution.py:69
  167.9 9.7 %copy-start.15 = (pred[256,256]{1,0:T(8,128)(4,1)}, pred[256,256]{1,0:T(8,128)(4,1)S(1)}, u32[]{:S(2)}) copy-start(pred[256,256]{1,0:T(8,128)(4,1)S(1)} %iota_compare_fusion.2) | copy-start | bytes 196612
  177.6 18.1 %copy-start.10 = (f32[256,32]{0,1:T(8,128)S(1)}, f32[256,32]{0,1:T(8,128)}, u32[]{:S(2)}) copy-start(f32[256,32]{0,1:T(8,128)} %copy-done.9) | copy-start | bytes 98308
  177.6 18.1 %copy-start.16 = (f32[2,16,256]{2,1,0:T(8,128)S(1)}, f32[2,16,256]{2,1,0:T(8,128)}, u32[]{:S(2)}) copy-start(f32[2,16,256]{2,1,0:T(8,128)} %get-tuple-element.63) | copy-start | bytes 98308
  177.6 5.6 %collective-permute-start.8 = (f32[2,16]{1,0:T(2,128)S(1)}, f32[2,16]{1,0:T(2,128)S(1)}, u32[]{:S(2)}, u32[]{:S(2)}) collective-permute-start(f32[2,16]{1,0:T(2,128)S(1)} %get-tuple-element.40), channel_id=1, source_target_pairs={{0,16},{2,18},{4,20},{6,22},{8,24},{10,26},{12,28},{14,30},{16,32}... | collective-permute-start | bytes 392 | tf_op jit(solution)/shard_map/ppermute | solution.py:69
  189.1 24.3 %collective-permute-start.9 = (f32[2,16,64,128]{3,2,1,0:T(8,128)}, f32[2,16,64,128]{3,2,1,0:T(8,128)}, u32[]{:S(2)}, u32[]{:S(2)}) collective-permute-start(f32[2,16,64,128]{3,2,1,0:T(8,128)} %multiply_add_fusion), channel_id=1, source_target_pairs={{0,64},{2,66},{4,68},{6,70},{8,72},{10,74},{12,76},{14,78},{16,80}... | collective-permute-start | bytes 3145736 | tf_op jit(solution)/shard_map/ppermute | solution.py:69
  195.7 17.6 %copy-start.4 = (f32[2,16,64,128]{3,2,1,0:T(8,128)S(1)}, f32[2,16,64,128]{3,2,1,0:T(8,128)}, u32[]{:S(2)}) copy-start(f32[2,16,64,128]{3,2,1,0:T(8,128)} %copy-done.3) | copy-start | bytes 3145732
  195.7 17.7 %copy-start.8 = (bf16[512,2,128]{2,1,0:T(2,128)(2,1)S(1)}, bf16[512,2,128]{2,1,0:T(2,128)(2,1)}, u32[]{:S(2)}) copy-start(bf16[512,2,128]{2,1,0:T(2,128)(2,1)} %reshape.266) | copy-start | bytes 786436
  195.7 17.7 %copy-start.14 = (f32[512,2,16]{0,2,1:T(8,128)S(1)}, f32[512,2,16]{0,2,1:T(8,128)}, u32[]{:S(2)}) copy-start(f32[512,2,16]{0,2,1:T(8,128)} %bitcast_bitcast_fusion) | copy-start | bytes 196612
  205.7 7.7 %collective-permute-start.10 = (f32[2,16]{1,0:T(2,128)}, f32[2,16]{1,0:T(2,128)S(1)}, u32[]{:S(2)}, u32[]{:S(2)}) collective-permute-start(f32[2,16]{1,0:T(2,128)} %get-tuple-element.38), channel_id=1, source_target_pairs={{0,32},{2,34},{4,36},{6,38},{8,40},{10,42},{12,44},{14,46},{16,48}... | collective-permute-start | bytes 392 | tf_op jit(solution)/shard_map/ppermute | solution.py:69
  227.8 97.1 %copy-start.2 = (bf16[512,2048]{1,0:T(8,128)(2,1)S(1)}, bf16[512,2048]{1,0:T(8,128)(2,1)}, u32[]{:S(2)}) copy-start(bf16[512,2048]{1,0:T(8,128)(2,1)} %param.19) | copy-start | bytes 6291460
  227.8 97.1 %copy-start.21 = (f32[2048]{0:T(1024)S(1)}, f32[2048]{0:T(1024)}, u32[]{:S(2)}) copy-start(f32[2048]{0:T(1024)} %param.25) | copy-start | bytes 24580
  354.3 0.7 copy-start.23
  354.3 0.9 copy-start.22
  354.3 26.6 %copy-start.19 = (s32[64]{0:T(128)S(1)}, s32[64]{0:T(128)}, u32[]{:S(2)}) copy-start(s32[64]{0:T(128)} %param.29) | copy-start | bytes 772
  354.3 26.6 %copy-start.20 = (s32[64]{0:T(128)S(1)}, s32[64]{0:T(128)}, u32[]{:S(2)}) copy-start(s32[64]{0:T(128)} %param.28) | copy-start | bytes 772
  375.8 26.4 %collective-permute-start.11 = (bf16[128,4096]{1,0:T(8,128)(2,1)S(1)}, bf16[128,4096]{1,0:T(8,128)(2,1)}, u32[]{:S(2)}, u32[]{:S(2)}) collective-permute-start(bf16[128,4096]{1,0:T(8,128)(2,1)S(1)} %slice.173), channel_id=1, source_target_pairs={{2,0},{4,2},{6,4},{8,6},{10,8},{12,10},{14,12},{16,14},{18,16},{20... | collective-permute-start | bytes 3145736 | tf_op jit(solution)/shard_map/ppermute | solution.py:14
  440.6 3.9 collective-permute-start.12
Sparse Core Ops, SparseCore 0:
  10.7 314.2 all-gather.1
  354.5 19.9 reduce-scatter.1

commit v2 on v1

--- a/solution.py
+++ b/solution.py
@@ -76,6 +76,14 @@
 def combine_states(earlier, later):
     return (earlier[0] * jnp.exp(later[1])[..., None, None] + later[0], earlier[1] + later[1])
 
+
+def head_sum(part, axis):
+    half = part.shape[1] // 2
+    me = lax.axis_index(axis)
+    mine = lax.dynamic_slice_in_dim(part, me * half, half, axis=1)
+    other = lax.dynamic_slice_in_dim(part, (1 - me) * half, half, axis=1)
+    got = lax.ppermute(other, axis, [(0, 1), (1, 0)])
+    return (mine.astype(jnp.float32) + got.astype(jnp.float32)).astype(jnp.bfloat16)
 
 def inside_mask(first, length, place):
     return jnp.logical_and(
@@ -123,21 +131,20 @@
     meansq = jnp.mean(gated * gated, axis=-1, keepdims=True)
     normalized_input = gated * lax.rsqrt(meansq + 1e-05)
     y_out = (normalized_input.reshape(tok, -1) * norm_gain[None, :]).astype(jnp.bfloat16)
+    reach = min(tok, 128)
+    next_rows = from_behind(y_out[:reach], "seq", -1)
+    extended = jnp.concatenate([y_out, next_rows], axis=0)
     partial_out = jnp.dot(
-        y_out,
+        extended,
         lax.all_gather(out_weight, "seq", axis=1, tiled=True),
         preferred_element_type=jnp.float32,
     )
-    layer_out = lax.psum_scatter(
-        partial_out.astype(jnp.bfloat16), "head", scatter_dimension=1, tiled=True
-    )
+    projected = head_sum(partial_out.astype(jnp.bfloat16), "head")
+    layer_out = projected[:tok]
     base = lax.axis_index("seq") * tok
-    reach = min(tok, 128)
-    following = from_behind(layer_out[:reach], "seq", -1)
-    rows = jnp.concatenate([layer_out, following], axis=0)
     place = base + jnp.arange(tok + reach, dtype=jnp.int32)
     sums = jnp.dot(
-        inside_mask(span_start, span_len, place), rows, preferred_element_type=jnp.float32
+        inside_mask(span_start, span_len, place), projected, preferred_element_type=jnp.float32
     )
     own_feature = (sums / span_len[:, None].astype(jnp.float32)).astype(jnp.bfloat16)
     count = span_start.shape[0]

time: 455 us -> 434 us (0.954)
  blocking collectives: 30.8 us -> 0 us
  waiting for transfers between devices: 194 us -> 181 us
  local copies, waits for them, and re-layouts: 43.2 us -> 54.3 us
  other arithmetic: 26.8 us -> 36.1 us
  starting transfers between devices: 68.6 us -> 76.7 us
  matrix products: 74.5 us -> 68.4 us
    all_to_all x1 -> x0, blocking collectives: 30.8 us -> none  [on_device(): got = lax.all_to_all(send, 'seq', split_axis=0, concat_axis=0, tiled=True)]
    reduce_scatter x1 -> x0, waiting for transfers between devices: 18.7 us -> none  [on_device(): lax.psum_scatter(partial_out.astype(jnp.bfloat16), 'head', scatter_dimens...]
    all_gather x1, waiting for transfers between devices: 91.6 us -> 74.3 us  [on_device(): lax.all_gather(out_weight, 'seq', axis=1, tiled=True)]
    all_to_all x0 -> x1, waiting for transfers between devices: none -> 13.1 us  [on_device(): got = lax.all_to_all(send, 'seq', split_axis=0, concat_axis=0, tiled=True)]
    convert_element_type x0 -> x2, other arithmetic: none -> 11.3 us  [the longest x1 6.13 us: head_sum(): (mine.astype(jnp.float32) + got.astype(jnp.float32)).astype(jnp.bfloat16)]
    all_to_all x0 -> x1, starting transfers between devices: none -> 8.61 us  [on_device(): got = lax.all_to_all(send, 'seq', split_axis=0, concat_axis=0, tiled=True)]
    unnamed x53 -> x59, local copies, waits for them, and re-layouts: 7.17 us -> 13.4 us
    dot_general x2, matrix products: 32.9 us -> 27.4 us  [the longest x1 26.3 us: on_device(): jnp.dot(extended, lax.all_gather(out_weight, 'seq', axis=1, tiled=True),...]
  transfers between devices with their start and end apart: 15 -> 16, of which waited for: 9 -> 10; matrix products, arithmetic and copies ran while one was open for 23% -> 25% of each run, Pallas kernels for 0% -> 0%
where the time goes in v2:
time: 434 us; the launch traced here: 432 us
  waiting for transfers between devices  181 us (42%)
  starting transfers between devices  76.7 us (18%)
  matrix products  68.4 us (16%)
  local copies, waits for them, and re-layouts  54.3 us (13%)
  other arithmetic  36.1 us (8%)
  between operations  15.3 us (4%)
    all_gather x1, waiting for transfers between devices, on_device(): lax.all_gather(out_weight, 'seq', axis=1, tiled=True)  74.3 us
    ppermute x11, waiting for transfers between devices, exclusive_scan(): got = jax.tree.map(lambda a: lax.ppermute(a, axis, pairs), inclusive)  64.4 us
    ppermute x11, starting transfers between devices, exclusive_scan(): got = jax.tree.map(lambda a: lax.ppermute(a, axis, pairs), inclusive)  62.3 us
    dot_general x1, matrix products, on_device(): jnp.dot(extended, lax.all_gather(out_weight, 'seq', axis=1, tiled=True),...  26.3 us
    ppermute x1, waiting for transfers between devices, from_behind(): lax.ppermute(value, axis, [(source, source + steps) for source in range(l...  23.8 us
    dot_general x2, matrix products, segment_summands(): intra = jnp.einsum('gkts,sgkp->tgkp', weights, xs, precision=high)  18.7 us
    dot_general x3, matrix products, inter_term(): jnp.einsum('tgn,gkpn->tgkp', cmat, state_in, precision=high)  14.1 us
    unnamed x59, local copies, waits for them, and re-layouts  13.4 us
  transfers between devices with their start and end apart: 16, of which 10 were waited for; matrix products, arithmetic and copies ran while one was open for 25% of the time, Pallas kernels for 0%

profile of v2, /device:TPU:1, one launch (start us, length us, event | category | flops | bytes accessed | tf_op | source)
XLA Modules:
  0.0 432.4 jit_solution(1797000068494222372)
XLA Ops:
  11.5 2.7 fusion.105
  15.7 2.0 fusion.107
  24.3 2.6 fusion.46
  26.9 4.4 %collective-permute-start = (f32[2,16,64,128]{3,2,1,0:T(8,128)S(1)}, f32[2,16,64,128]{3,2,1,0:T(8,128)S(1)}, u32[]{:S(2)}, u32[]{:S(2)}) collective-permute-start(f32[2,16,64,128]{3,2,1,0:T(8,128)S(1)} %fusion.46), channel_id=1, source_target_pairs={{0,2},{2,4},{4,6},{6,8},{8,10},{10,12},{12,14},{14,16},{16,18},{18... | collective-permute-start | bytes 3145736 | tf_op jit(solution)/shard_map/ppermute | solution.py:69
  31.3 21.8 %collective-permute-done = f32[2,16,64,128]{3,2,1,0:T(8,128)S(1)} collective-permute-done((f32[2,16,64,128]{3,2,1,0:T(8,128)S(1)}, f32[2,16,64,128]{3,2,1,0:T(8,128)S(1)}, u32[]{:S(2)}, u32[]{:S(2)}) %collective-permute-start) | collective-permute-done | bytes 1048608 | tf_op jit(solution)/shard_map/ppermute | solution.py:69
  53.2 6.1 %collective-permute-start.1 = (f32[2,16,64,128]{3,2,1,0:T(8,128)S(1)}, f32[2,16,64,128]{3,2,1,0:T(8,128)S(1)}, u32[]{:S(2)}, u32[]{:S(2)}) collective-permute-start(f32[2,16,64,128]{3,2,1,0:T(8,128)S(1)} %multiply_add_fusion.4), channel_id=1, source_target_pairs={{0,4},{2,6},{4,8},{6,10},{8,12},{10,14},{12,16},{14,18},{16,20},{1... | collective-permute-start | bytes 3145736 | tf_op jit(solution)/shard_map/ppermute | solution.py:69
  59.3 6.4 %collective-permute-start.2 = (f32[2,16]{1,0:T(2,128)S(1)}, f32[2,16]{1,0:T(2,128)S(1)}, u32[]{:S(2)}, u32[]{:S(2)}) collective-permute-start(f32[2,16]{1,0:T(2,128)S(1)} %get-tuple-element.46), channel_id=1, source_target_pairs={{0,2},{2,4},{4,6},{6,8},{8,10},{10,12},{12,14},{14,16},{16,18},{18... | collective-permute-start | bytes 392 | tf_op jit(solution)/shard_map/ppermute | solution.py:69
  65.7 27.8 %collective-permute-done.2 = f32[2,16]{1,0:T(2,128)S(1)} collective-permute-done((f32[2,16]{1,0:T(2,128)S(1)}, f32[2,16]{1,0:T(2,128)S(1)}, u32[]{:S(2)}, u32[]{:S(2)}) %collective-permute-start.2) | collective-permute-done | bytes 160 | tf_op jit(solution)/shard_map/ppermute | solution.py:69
  94.3 7.3 %collective-permute-start.3 = (f32[2,16,64,128]{3,2,1,0:T(8,128)S(1)}, f32[2,16,64,128]{3,2,1,0:T(8,128)}, u32[]{:S(2)}, u32[]{:S(2)}) collective-permute-start(f32[2,16,64,128]{3,2,1,0:T(8,128)S(1)} %multiply_add_fusion.3), channel_id=1, source_target_pairs={{0,8},{2,10},{4,12},{6,14},{8,16},{10,18},{12,20},{14,22},{16,24},... | collective-permute-start | bytes 3145736 | tf_op jit(solution)/shard_map/ppermute | solution.py:69
  104.8 5.1 %reduce-window.26 = f32[16,2,4,128]{3,0,1,2:T(8,128)} reduce-window(f32[16,2,4,128]{3,0,1,2:T(8,128)} %bitcast.166, f32[]{:T(128)} %constant.90.clone.1), window={size=1x1x1x128 pad=0_0x0_0x0_0x127_0}, to_apply=%region_4.5 | reduce-window | flops 2080768 | bytes 131076 | tf_op jit(solution)/shard_map/reduce-window.4
  112.5 1.6 bitcast_bitcast_fusion
  115.1 5.0 %collective-permute-start.4 = (f32[2,16]{1,0:T(2,128)}, f32[2,16]{1,0:T(2,128)S(1)}, u32[]{:S(2)}, u32[]{:S(2)}) collective-permute-start(f32[2,16]{1,0:T(2,128)} %get-tuple-element.44), channel_id=1, source_target_pairs={{0,4},{2,6},{4,8},{6,10},{8,12},{10,14},{12,16},{14,18},{16,20},{1... | collective-permute-start | bytes 392 | tf_op jit(solution)/shard_map/ppermute | solution.py:69
  121.8 2.3 multiply_add_fusion.2
  124.1 8.4 %collective-permute-start.5 = (f32[2,16,64,128]{3,2,1,0:T(8,128)}, f32[2,16,64,128]{3,2,1,0:T(8,128)S(1)}, u32[]{:S(2)}, u32[]{:S(2)}) collective-permute-start(f32[2,16,64,128]{3,2,1,0:T(8,128)} %multiply_add_fusion.2), channel_id=1, source_target_pairs={{0,16},{2,18},{4,20},{6,22},{8,24},{10,26},{12,28},{14,30},{16,32}... | collective-permute-start | bytes 3145736 | tf_op jit(solution)/shard_map/ppermute | solution.py:69
  133.6 2.3 fusion.75
  135.9 2.3 fusion.113
  138.2 2.7 collective-permute-start.6
  141.0 4.2 copy.158
  146.0 6.8 %collective-permute-done.6 = f32[2,16]{1,0:T(2,128)S(1)} collective-permute-done((f32[2,16]{1,0:T(2,128)S(1)}, f32[2,16]{1,0:T(2,128)S(1)}, u32[]{:S(2)}, u32[]{:S(2)}) %collective-permute-start.6) | collective-permute-done | bytes 160 | tf_op jit(solution)/shard_map/ppermute | solution.py:69
  152.8 2.7 multiply_add_fusion.1
  155.5 10.5 %collective-permute-start.7 = (f32[2,16,64,128]{3,2,1,0:T(8,128)}, f32[2,16,64,128]{3,2,1,0:T(8,128)}, u32[]{:S(2)}, u32[]{:S(2)}) collective-permute-start(f32[2,16,64,128]{3,2,1,0:T(8,128)} %multiply_add_fusion.1), channel_id=1, source_target_pairs={{0,32},{2,34},{4,36},{6,38},{8,40},{10,42},{12,44},{14,46},{16,48}... | collective-permute-start | bytes 3145736 | tf_op jit(solution)/shard_map/ppermute | solution.py:69
  166.1 9.3 %fusion.31 = f32[256,2,16,64]{0,3,2,1:T(8,128)} fusion(f32[2,16,64,256]{3,2,1,0:T(8,128)} %fusion.113, bf16[256,2,16,64]{0,3,2,1:T(8,128)(2,1)} %bitcast.155, f32[2,16,256]{2,1,0:T(8,128)S(1)} %bitcast.174, f32[2,16,256]{2,1,0:T(8,128)S(1)} %copy-done.20, f32[2,256,256]{2,1,0:T(8,128)} %fusion.112, pred[256,256]{1,0:T(8,128)(4,1)S(1)} %iota_compare_fusion.2, ...), kind=kOutput, calls=%fused_computation.41 | convolution fusion | flops 1622147072 | bytes 5931008 | tf_op jit(solution)/shard_map/gkts,sgkp->tgkp/dot_general | solution.py:26
  175.4 1.6 collective-permute-start.8
  177.0 2.9 copy.160
  180.5 3.9 collective-permute-done.7
  184.4 2.7 multiply_add_fusion
  187.2 6.5 %collective-permute-start.9 = (f32[2,16,64,128]{3,2,1,0:T(8,128)}, f32[2,16,64,128]{3,2,1,0:T(8,128)}, u32[]{:S(2)}, u32[]{:S(2)}) collective-permute-start(f32[2,16,64,128]{3,2,1,0:T(8,128)} %multiply_add_fusion), channel_id=1, source_target_pairs={{0,64},{2,66},{4,68},{6,70},{8,72},{10,74},{12,76},{14,78},{16,80}... | collective-permute-start | bytes 3145736 | tf_op jit(solution)/shard_map/ppermute | solution.py:69
  193.7 9.5 %fusion.32 = f32[256,2,16,64]{0,3,2,1:T(8,128)} fusion(f32[2,16,64,256]{3,2,1,0:T(8,128)} %fusion.75, bf16[256,2,16,64]{0,3,2,1:T(8,128)(2,1)} %bitcast.153, f32[2,16,256]{2,1,0:T(8,128)S(1)} %bitcast.172, f32[2,16,256]{2,1,0:T(8,128)S(1)} %copy-done.19, f32[2,256,256]{2,1,0:T(8,128)} %fusion.111, pred[256,256]{1,0:T(8,128)(4,1)} %copy-done.18, ...), kind=kOutput, calls=%fused_computation.43 | convolution fusion | flops 1622147072 | bytes 5931008 | tf_op jit(solution)/shard_map/gkts,sgkp->tgkp/dot_general | solution.py:26
  203.2 3.2 collective-permute-start.10
  207.2 4.1 collective-permute-done.10
  211.3 9.5 %multiply_reduce_fusion = (f32[512,2]{0,1:T(2,128)S(1)}, f32[512,2,16,64]{0,3,2,1:T(8,128)}) fusion(f32[512,2048]{0,1:T(8,128)} %copy.160, f32[512,2,16,64]{0,3,2,1:T(8,128)} %bitcast.150, f32[2,16]{1,0:T(2,128)S(1)} %mul.261, bf16[512,2,128,1]{2,1,0,3:T(2,128)(2,1)S(1)} %bitcast.164, f32[2,16,64,128]{3,2,1,0:T(8,128)} %copy-done.6, ...), kind=kOutput, calls=%fused_computation.24 | convolution fusion | flops 1625816064 | bytes 23401216 | tf_op jit(solution)/shard_map/tgn,gkpn->tgkp/dot_general | solution.py:34
  222.1 4.0 copy.192
  226.1 5.5 %copy.159 = f32[512,2048]{1,0:T(8,128)} copy(f32[512,2048]{0,1:T(8,128)} %bitcast.151) | data formatting | bytes 8388608 | tf_op jit(solution)/shard_map/reshape | solution.py:127
  231.6 5.1 %multiply_convert_fusion = bf16[512,2048]{1,0:T(8,128)(2,1)S(1)} fusion(f32[512,2048]{1,0:T(8,128)} %bitcast.149, f32[512,2048]{1,0:T(8,128)} %copy.159, f32[2048]{0:T(1024)S(1)} %copy-done.22, bf16[512,2048]{1,0:T(8,128)(2,1)S(1)} %copy-done.3), kind=kLoop, calls=%fused_computation.23 | loop fusion | flops 9437184 | bytes 12591104 | tf_op jit(solution)/shard_map/convert_element_type | solution.py:133
  239.6 23.8 %collective-permute-done.11 = bf16[128,2048]{1,0:T(8,128)(2,1)S(1)} collective-permute-done((bf16[128,2048]{1,0:T(8,128)(2,1)S(1)}, bf16[128,2048]{1,0:T(8,128)(2,1)S(1)}, u32[]{:S(2)}, u32[]{:S(2)}) %collective-permute-start.11) | collective-permute-done | bytes 524320 | tf_op jit(solution)/shard_map/ppermute | solution.py:14
  263.4 74.3 %all-gather.2.cloned.1.call-done = bf16[2048,8192]{1,0:T(8,128)(2,1)} async-done(((bf16[2048,128]{1,0:T(8,128)(2,1)}), bf16[2048,8192]{1,0:T(8,128)(2,1)}) %all-gather.2.cloned.1.call-update) | async-done | bytes 33554448 | tf_op jit(solution)/shard_map/all_gather | solution.py:139
  337.7 26.3 %convolution_convert_fusion = bf16[640,8192]{1,0:T(8,128)(2,1)S(1)} fusion(bf16[2048,8192]{1,0:T(8,128)(2,1)} %all-gather.2.cloned.1.call-done, bf16[128,2048]{1,0:T(8,128)(2,1)S(1)} %collective-permute-done.11, bf16[512,2048]{1,0:T(8,128)(2,1)} %copy-done.5), kind=kOutput, calls=%fused_computation.1 | convolution fusion | flops 21485322240 | bytes 46661632 | tf_op jit(solution)/shard_map/dot_general | solution.py:137
  364.1 2.9 constant_dynamic-slice_fusion
  367.0 2.7 copy-done.2
  369.6 2.0 collective-permute-start.12
  376.0 4.3 collective-permute-done.12
  380.3 6.1 %add_convert_fusion = bf16[640,4096]{1,0:T(8,128)(2,1)S(1)} fusion(bf16[640,4096]{1,0:T(8,128)(2,1)} %collective-permute-done.12, bf16[640,8192]{1,0:T(8,128)(2,1)} %copy-done.2, s32[]{:T(128)S(6)} %select_n.53), kind=kLoop, calls=%fused_computation.2 | loop fusion | flops 10485760 | bytes 15728644 | tf_op jit(solution)/shard_map/convert_element_type | solution.py:86
  386.4 2.3 copy-done.1
  392.4 8.6 %all-to-all-start = ((bf16[64,2,4224]{2,1,0:T(2,128)(2,1)}), bf16[64,2,4224]{2,1,0:T(2,128)(2,1)S(1)}, u32[]{:S(2)}, u32[]{:S(2)}) async-start(bf16[64,2,4224]{2,1,0:T(2,128)(2,1)} %reshape.274), calls=%async_computation | async-start | bytes 2162688 | tf_op jit(solution)/shard_map/all_to_all | solution.py:168
  401.0 4.7 %slice.178 = bf16[512,4096]{1,0:T(8,128)(2,1)} slice(bf16[640,4096]{1,0:T(8,128)(2,1)} %copy-done.1), slice={[0:512], [0:4096]} | slice | bytes 8388608 | tf_op jit(solution)/shard_map/slice | solution.py:143
  405.7 13.1 %all-to-all-done = bf16[64,2,4224]{2,1,0:T(2,128)(2,1)S(1)} async-done(((bf16[64,2,4224]{2,1,0:T(2,128)(2,1)}), bf16[64,2,4224]{2,1,0:T(2,128)(2,1)S(1)}, u32[]{:S(2)}, u32[]{:S(2)}) %all-to-all-start) | async-done | bytes 1081376 | tf_op jit(solution)/shard_map/all_to_all | solution.py:168
  420.0 2.2 collective-permute-start.13
  423.7 1.8 convolution_bitcast_fusion
  (141 shorter events, 38.9 us)
Async XLA Ops:
  7.2 412.3 %copy-start = (bf16[1,4096,128]{2,1,0:T(8,128)(2,1)S(1)}, bf16[1,4096,128]{2,1,0:T(8,128)(2,1)}, u32[]{:S(2)}) copy-start(bf16[1,4096,128]{2,1,0:T(8,128)(2,1)} %param.27) | copy-start | bytes 3145732
  7.2 330.5 %all-gather.2.cloned.1.call-start = ((), (), s32[]{:S(2)}) async-start(), calls=%async_computation.1 | async-start | bytes 34078720 | tf_op jit(solution)/shard_map/all_gather | solution.py:139
  11.5 10.2 %copy-start.16 = (f32[512,32]{0,1:T(8,128)S(1)}, f32[512,32]{0,1:T(8,128)}, u32[]{:S(2)}) copy-start(f32[512,32]{0,1:T(8,128)} %param.22) | copy-start | bytes 196612
  15.7 11.1 %copy-start.4 = (bf16[256,2048]{0,1:T(8,128)(2,1)}, bf16[256,2048]{0,1:T(8,128)(2,1)S(1)}, u32[]{:S(2)}) copy-start(bf16[256,2048]{0,1:T(8,128)(2,1)S(1)} %copy.139) | copy-start | bytes 3145732
  21.7 1.4 copy-start.12
  21.7 2.6 copy-start.14
  24.3 77.3 %copy-start.9 = (bf16[512,256]{1,0:T(8,128)(2,1)S(1)}, bf16[512,256]{1,0:T(8,128)(2,1)}, u32[]{:S(2)}) copy-start(bf16[512,256]{1,0:T(8,128)(2,1)} %param.21) | copy-start | bytes 786436
  26.9 26.1 %collective-permute-start = (f32[2,16,64,128]{3,2,1,0:T(8,128)S(1)}, f32[2,16,64,128]{3,2,1,0:T(8,128)S(1)}, u32[]{:S(2)}, u32[]{:S(2)}) collective-permute-start(f32[2,16,64,128]{3,2,1,0:T(8,128)S(1)} %fusion.46), channel_id=1, source_target_pairs={{0,2},{2,4},{4,6},{6,8},{8,10},{10,12},{12,14},{14,16},{16,18},{18... | collective-permute-start | bytes 3145736 | tf_op jit(solution)/shard_map/ppermute | solution.py:69
  53.0 49.3 %copy-start.6 = (f32[2,16,64,128]{3,2,1,0:T(8,128)}, f32[2,16,64,128]{3,2,1,0:T(8,128)S(1)}, u32[]{:S(2)}) copy-start(f32[2,16,64,128]{3,2,1,0:T(8,128)S(1)} %collective-permute-done) | copy-start | bytes 3145732
  53.2 41.0 %collective-permute-start.1 = (f32[2,16,64,128]{3,2,1,0:T(8,128)S(1)}, f32[2,16,64,128]{3,2,1,0:T(8,128)S(1)}, u32[]{:S(2)}, u32[]{:S(2)}) collective-permute-start(f32[2,16,64,128]{3,2,1,0:T(8,128)S(1)} %multiply_add_fusion.4), channel_id=1, source_target_pairs={{0,4},{2,6},{4,8},{6,10},{8,12},{10,14},{12,16},{14,18},{16,20},{1... | collective-permute-start | bytes 3145736 | tf_op jit(solution)/shard_map/ppermute | solution.py:69
  59.3 34.2 %collective-permute-start.2 = (f32[2,16]{1,0:T(2,128)S(1)}, f32[2,16]{1,0:T(2,128)S(1)}, u32[]{:S(2)}, u32[]{:S(2)}) collective-permute-start(f32[2,16]{1,0:T(2,128)S(1)} %get-tuple-element.46), channel_id=1, source_target_pairs={{0,2},{2,4},{4,6},{6,8},{8,10},{10,12},{12,14},{14,16},{16,18},{18... | collective-permute-start | bytes 392 | tf_op jit(solution)/shard_map/ppermute | solution.py:69
  94.1 8.2 %copy-start.7 = (f32[2,16,64,128]{3,2,1,0:T(8,128)}, f32[2,16,64,128]{3,2,1,0:T(8,128)S(1)}, u32[]{:S(2)}) copy-start(f32[2,16,64,128]{3,2,1,0:T(8,128)S(1)} %collective-permute-done.1) | copy-start | bytes 3145732
  94.3 27.5 %collective-permute-start.3 = (f32[2,16,64,128]{3,2,1,0:T(8,128)S(1)}, f32[2,16,64,128]{3,2,1,0:T(8,128)}, u32[]{:S(2)}, u32[]{:S(2)}) collective-permute-start(f32[2,16,64,128]{3,2,1,0:T(8,128)S(1)} %multiply_add_fusion.3), channel_id=1, source_target_pairs={{0,8},{2,10},{4,12},{6,14},{8,16},{10,18},{12,20},{14,22},{16,24},... | collective-permute-start | bytes 3145736 | tf_op jit(solution)/shard_map/ppermute | solution.py:69
  115.1 6.0 %collective-permute-start.4 = (f32[2,16]{1,0:T(2,128)}, f32[2,16]{1,0:T(2,128)S(1)}, u32[]{:S(2)}, u32[]{:S(2)}) collective-permute-start(f32[2,16]{1,0:T(2,128)} %get-tuple-element.44), channel_id=1, source_target_pairs={{0,4},{2,6},{4,8},{6,10},{8,12},{10,14},{12,16},{14,18},{16,20},{1... | collective-permute-start | bytes 392 | tf_op jit(solution)/shard_map/ppermute | solution.py:69
  124.1 28.6 %collective-permute-start.5 = (f32[2,16,64,128]{3,2,1,0:T(8,128)}, f32[2,16,64,128]{3,2,1,0:T(8,128)S(1)}, u32[]{:S(2)}, u32[]{:S(2)}) collective-permute-start(f32[2,16,64,128]{3,2,1,0:T(8,128)} %multiply_add_fusion.2), channel_id=1, source_target_pairs={{0,16},{2,18},{4,20},{6,22},{8,24},{10,26},{12,28},{14,30},{16,32}... | collective-permute-start | bytes 3145736 | tf_op jit(solution)/shard_map/ppermute | solution.py:69
  135.9 9.3 %copy-start.10 = (bf16[512,256]{1,0:T(8,128)(2,1)S(1)}, bf16[512,256]{1,0:T(8,128)(2,1)}, u32[]{:S(2)}) copy-start(bf16[512,256]{1,0:T(8,128)(2,1)} %param.21) | copy-start | bytes 786436
  138.2 27.8 %copy-start.15 = (f32[256,32]{0,1:T(8,128)S(1)}, f32[256,32]{0,1:T(8,128)}, u32[]{:S(2)}) copy-start(f32[256,32]{0,1:T(8,128)} %copy-done.14) | copy-start | bytes 98308
  138.2 27.8 %copy-start.20 = (f32[2,16,256]{2,1,0:T(8,128)S(1)}, f32[2,16,256]{2,1,0:T(8,128)}, u32[]{:S(2)}) copy-start(f32[2,16,256]{2,1,0:T(8,128)} %get-tuple-element.60) | copy-start | bytes 98308
  138.2 27.8 %copy-start.21 = (f32[256,2,16]{0,2,1:T(8,128)S(1)}, f32[256,2,16]{0,2,1:T(8,128)}, u32[]{:S(2)}) copy-start(f32[256,2,16]{0,2,1:T(8,128)} %get-tuple-element.58) | copy-start | bytes 98308
  138.2 14.5 %collective-permute-start.6 = (f32[2,16]{1,0:T(2,128)S(1)}, f32[2,16]{1,0:T(2,128)S(1)}, u32[]{:S(2)}, u32[]{:S(2)}) collective-permute-start(f32[2,16]{1,0:T(2,128)S(1)} %get-tuple-element.42), channel_id=1, source_target_pairs={{0,8},{2,10},{4,12},{6,14},{8,16},{10,18},{12,20},{14,22},{16,24},... | collective-permute-start | bytes 392 | tf_op jit(solution)/shard_map/ppermute | solution.py:69
  152.8 13.3 %copy-start.8 = (f32[2,16,64,128]{3,2,1,0:T(8,128)}, f32[2,16,64,128]{3,2,1,0:T(8,128)S(1)}, u32[]{:S(2)}) copy-start(f32[2,16,64,128]{3,2,1,0:T(8,128)S(1)} %collective-permute-done.5) | copy-start | bytes 3145732
  155.5 28.9 %collective-permute-start.7 = (f32[2,16,64,128]{3,2,1,0:T(8,128)}, f32[2,16,64,128]{3,2,1,0:T(8,128)}, u32[]{:S(2)}, u32[]{:S(2)}) collective-permute-start(f32[2,16,64,128]{3,2,1,0:T(8,128)} %multiply_add_fusion.1), channel_id=1, source_target_pairs={{0,32},{2,34},{4,36},{6,38},{8,40},{10,42},{12,44},{14,46},{16,48}... | collective-permute-start | bytes 3145736 | tf_op jit(solution)/shard_map/ppermute | solution.py:69
  166.1 9.3 %copy-start.18 = (pred[256,256]{1,0:T(8,128)(4,1)}, pred[256,256]{1,0:T(8,128)(4,1)S(1)}, u32[]{:S(2)}) copy-start(pred[256,256]{1,0:T(8,128)(4,1)S(1)} %iota_compare_fusion.2) | copy-start | bytes 196612
  166.1 10.9 %copy-start.3 = (bf16[512,2048]{1,0:T(8,128)(2,1)S(1)}, bf16[512,2048]{1,0:T(8,128)(2,1)}, u32[]{:S(2)}) copy-start(bf16[512,2048]{1,0:T(8,128)(2,1)} %param.19) | copy-start | bytes 6291460
  175.4 18.3 %copy-start.13 = (f32[256,32]{0,1:T(8,128)S(1)}, f32[256,32]{0,1:T(8,128)}, u32[]{:S(2)}) copy-start(f32[256,32]{0,1:T(8,128)} %copy-done.12) | copy-start | bytes 98308
  175.4 18.3 %copy-start.19 = (f32[2,16,256]{2,1,0:T(8,128)S(1)}, f32[2,16,256]{2,1,0:T(8,128)}, u32[]{:S(2)}) copy-start(f32[2,16,256]{2,1,0:T(8,128)} %get-tuple-element.63) | copy-start | bytes 98308
  175.4 4.6 %collective-permute-start.8 = (f32[2,16]{1,0:T(2,128)S(1)}, f32[2,16]{1,0:T(2,128)S(1)}, u32[]{:S(2)}, u32[]{:S(2)}) collective-permute-start(f32[2,16]{1,0:T(2,128)S(1)} %get-tuple-element.40), channel_id=1, source_target_pairs={{0,16},{2,18},{4,20},{6,22},{8,24},{10,26},{12,28},{14,30},{16,32}... | collective-permute-start | bytes 392 | tf_op jit(solution)/shard_map/ppermute | solution.py:69
  187.2 24.1 %collective-permute-start.9 = (f32[2,16,64,128]{3,2,1,0:T(8,128)}, f32[2,16,64,128]{3,2,1,0:T(8,128)}, u32[]{:S(2)}, u32[]{:S(2)}) collective-permute-start(f32[2,16,64,128]{3,2,1,0:T(8,128)} %multiply_add_fusion), channel_id=1, source_target_pairs={{0,64},{2,66},{4,68},{6,70},{8,72},{10,74},{12,76},{14,78},{16,80}... | collective-permute-start | bytes 3145736 | tf_op jit(solution)/shard_map/ppermute | solution.py:69
  193.7 17.6 %copy-start.11 = (bf16[512,2,128]{2,1,0:T(2,128)(2,1)S(1)}, bf16[512,2,128]{2,1,0:T(2,128)(2,1)}, u32[]{:S(2)}) copy-start(bf16[512,2,128]{2,1,0:T(2,128)(2,1)} %reshape.266) | copy-start | bytes 786436
  193.7 17.6 %copy-start.17 = (f32[512,2,16]{0,2,1:T(8,128)S(1)}, f32[512,2,16]{0,2,1:T(8,128)}, u32[]{:S(2)}) copy-start(f32[512,2,16]{0,2,1:T(8,128)} %bitcast_bitcast_fusion) | copy-start | bytes 196612
  203.2 8.1 %collective-permute-start.10 = (f32[2,16]{1,0:T(2,128)}, f32[2,16]{1,0:T(2,128)S(1)}, u32[]{:S(2)}, u32[]{:S(2)}) collective-permute-start(f32[2,16]{1,0:T(2,128)} %get-tuple-element.38), channel_id=1, source_target_pairs={{0,32},{2,34},{4,36},{6,38},{8,40},{10,42},{12,44},{14,46},{16,48}... | collective-permute-start | bytes 392 | tf_op jit(solution)/shard_map/ppermute | solution.py:69
  226.1 5.5 %copy-start.22 = (f32[2048]{0:T(1024)S(1)}, f32[2048]{0:T(1024)}, u32[]{:S(2)}) copy-start(f32[2048]{0:T(1024)} %param.25) | copy-start | bytes 24580
  236.7 1.3 copy-start.5
  238.1 25.4 %collective-permute-start.11 = (bf16[128,2048]{1,0:T(8,128)(2,1)S(1)}, bf16[128,2048]{1,0:T(8,128)(2,1)S(1)}, u32[]{:S(2)}, u32[]{:S(2)}) collective-permute-start(bf16[128,2048]{1,0:T(8,128)(2,1)S(1)} %slice.177), channel_id=1, source_target_pairs={{2,0},{4,2},{6,4},{8,6},{10,8},{12,10},{14,12},{16,14},{18,16},{20... | collective-permute-start | bytes 1572872 | tf_op jit(solution)/shard_map/ppermute | solution.py:14
  364.0 5.6 %copy-start.2 = (bf16[640,8192]{1,0:T(8,128)(2,1)}, bf16[640,8192]{1,0:T(8,128)(2,1)S(1)}, u32[]{:S(2)}) copy-start(bf16[640,8192]{1,0:T(8,128)(2,1)S(1)} %convolution_convert_fusion) | copy-start | bytes 31457284
  364.0 8.9 %copy-start.25 = (s32[64]{0:T(128)S(1)}, s32[64]{0:T(128)}, u32[]{:S(2)}) copy-start(s32[64]{0:T(128)} %param.31) | copy-start | bytes 772
  364.1 11.0 %copy-start.26 = (s32[64,1]{0,1:T(1,128)S(1)}, s32[64,1]{0,1:T(1,128)}, u32[]{:S(2)}) copy-start(s32[64,1]{0,1:T(1,128)} %param.30) | copy-start | bytes 772
  364.1 11.9 %copy-start.23 = (s32[64]{0:T(128)S(1)}, s32[64]{0:T(128)}, u32[]{:S(2)}) copy-start(s32[64]{0:T(128)} %param.29) | copy-start | bytes 772
  364.1 11.9 %copy-start.24 = (s32[64]{0:T(128)S(1)}, s32[64]{0:T(128)}, u32[]{:S(2)}) copy-start(s32[64]{0:T(128)} %param.28) | copy-start | bytes 772
  369.6 10.7 %collective-permute-start.12 = (bf16[640,4096]{1,0:T(8,128)(2,1)}, bf16[640,4096]{1,0:T(8,128)(2,1)}, u32[]{:S(2)}, u32[]{:S(2)}) collective-permute-start(bf16[640,4096]{1,0:T(8,128)(2,1)} %constant_dynamic-slice_fusion), channel_id=1, source_target_pairs={{0,1},{1,0},{2,3},{3,2},{4,5},{5,4},{6,7},{7,6},{8,9},{9,8},{10,11... | collective-permute-start | bytes 15728648 | tf_op jit(solution)/shard_map/ppermute | solution.py:85
  386.4 2.3 copy-start.1
  392.4 26.5 %all-to-all-start = ((bf16[64,2,4224]{2,1,0:T(2,128)(2,1)}), bf16[64,2,4224]{2,1,0:T(2,128)(2,1)S(1)}, u32[]{:S(2)}, u32[]{:S(2)}) async-start(bf16[64,2,4224]{2,1,0:T(2,128)(2,1)} %reshape.274), calls=%async_computation | async-start | bytes 2162688 | tf_op jit(solution)/shard_map/all_to_all | solution.py:168
  420.0 3.1 collective-permute-start.13
Sparse Core Ops, SparseCore 0:
  10.7 326.9 all-gather.1

commit v3 on v2

--- a/solution.py
+++ b/solution.py
@@ -1,11 +1,12 @@
 import jax
 import jax.numpy as jnp
 from jax import lax
-from jax.sharding import PartitionSpec as P
+from jax.sharding import Mesh, PartitionSpec as P
 
 HEAD_DIM = 64
 STATE = 128
 CAP = 2
+SEQ = ("plane", "z")
 
 
 def from_behind(value, axis, steps):
@@ -84,6 +85,28 @@
     other = lax.dynamic_slice_in_dim(part, (1 - me) * half, half, axis=1)
     got = lax.ppermute(other, axis, [(0, 1), (1, 0)])
     return (mine.astype(jnp.float32) + got.astype(jnp.float32)).astype(jnp.bfloat16)
+
+
+def grouped_projection(y_out, out_weight, reach):
+    tok = y_out.shape[0]
+    groups = lax.axis_size("z")
+    planes = lax.axis_size("plane")
+    gathered_weight = lax.all_gather(out_weight, "plane", axis=1, tiled=True)
+    group_rows = lax.all_gather(y_out, "z", axis=0, tiled=True)
+    first = y_out[:reach]
+    extra = None
+    for target in range(groups):
+        pairs = [((p + 1) * groups, p * groups + target) for p in range(planes - 1)]
+        got = lax.ppermute(first, SEQ, pairs)
+        extra = got if extra is None else extra + got
+    extended = jnp.concatenate([group_rows, extra], axis=0)
+    part = jnp.dot(extended, gathered_weight, preferred_element_type=jnp.float32)
+    summed = head_sum(part.astype(jnp.bfloat16), "head")
+    send = jnp.stack([summed[z * tok : z * tok + tok + reach] for z in range(groups)])
+    back = lax.all_to_all(send, "z", 0, 0, tiled=True)
+    blocks = summed.shape[1] // 128
+    back = back.reshape(groups, tok + reach, blocks, 128)
+    return jnp.transpose(back, (1, 2, 0, 3)).reshape(tok + reach, groups * blocks * 128)
 
 def inside_mask(first, length, place):
     return jnp.logical_and(
@@ -118,7 +141,7 @@
     logd = log_decay.reshape(tok, groups_here, per_group)
     cum = jnp.cumsum(logd, axis=0)
     intra, local_state, total = piecewise_terms(xs, bmat, cmat, dtk, logd)
-    state_in = exclusive_scan((local_state, total), "seq")
+    state_in = exclusive_scan((local_state, total), SEQ)
     ssm = (
         intra
         + inter_term(cmat, cum, state_in)
@@ -132,23 +155,16 @@
     normalized_input = gated * lax.rsqrt(meansq + 1e-05)
     y_out = (normalized_input.reshape(tok, -1) * norm_gain[None, :]).astype(jnp.bfloat16)
     reach = min(tok, 128)
-    next_rows = from_behind(y_out[:reach], "seq", -1)
-    extended = jnp.concatenate([y_out, next_rows], axis=0)
-    partial_out = jnp.dot(
-        extended,
-        lax.all_gather(out_weight, "seq", axis=1, tiled=True),
-        preferred_element_type=jnp.float32,
-    )
-    projected = head_sum(partial_out.astype(jnp.bfloat16), "head")
+    projected = grouped_projection(y_out, out_weight, reach)
     layer_out = projected[:tok]
-    base = lax.axis_index("seq") * tok
+    base = lax.axis_index(SEQ) * tok
     place = base + jnp.arange(tok + reach, dtype=jnp.int32)
     sums = jnp.dot(
         inside_mask(span_start, span_len, place), projected, preferred_element_type=jnp.float32
     )
     own_feature = (sums / span_len[:, None].astype(jnp.float32)).astype(jnp.bfloat16)
     count = span_start.shape[0]
-    owners = lax.axis_size("seq")
+    owners = lax.axis_size(SEQ)
     slots_total = owners * CAP
     owner = span_owner[:, 0]
     index = jnp.arange(count)
@@ -165,7 +181,7 @@
     empty = jnp.zeros((1, packed.shape[1]), jnp.bfloat16).at[0, width].set(-1.0)
     chosen = jnp.where(jnp.any(pick, axis=1), jnp.argmax(pick, axis=1), count)
     send = jnp.concatenate([packed, empty], axis=0)[chosen].reshape(owners, CAP, -1)
-    got = lax.all_to_all(send, "seq", split_axis=0, concat_axis=0, tiled=True)
+    got = lax.all_to_all(send, SEQ, split_axis=0, concat_axis=0, tiled=True)
     got = got.reshape(slots_total, -1)
     feature = got[:, :width]
     labels = got[:, width].astype(jnp.int32)
@@ -185,25 +201,28 @@
 
 def solution(mesh):
     placed = (
-        P("seq", "head"),
-        P("seq", "head"),
-        P("seq", "head"),
-        P("seq", "head"),
-        P("seq", "head"),
-        P("seq", "head"),
+        P(SEQ, "head"),
+        P(SEQ, "head"),
+        P(SEQ, "head"),
+        P(SEQ, "head"),
+        P(SEQ, "head"),
+        P(SEQ, "head"),
         P("head"),
         P("head"),
-        P("head", "seq"),
-        P("seq", "head", None),
-        P("seq"),
-        P("seq"),
-        P("seq", None),
-        P("seq"),
-    )
+        P("head", SEQ),
+        P(SEQ, "head", None),
+        P(SEQ),
+        P(SEQ),
+        P(SEQ, None),
+        P(SEQ),
+    )
+    seq_count, head_count = mesh.devices.shape
+    group = 4 if seq_count % 4 == 0 else 1
+    grid = Mesh(mesh.devices.reshape(seq_count // group, group, head_count), ("plane", "z", "head"))
     return jax.shard_map(
         on_device,
-        mesh=mesh,
+        mesh=grid,
         in_specs=placed,
-        out_specs=(P("seq", "head"), P("seq", "head", None), P("seq", None)),
+        out_specs=(P(SEQ, "head"), P(SEQ, "head", None), P(SEQ, None)),
         check_vma=False,
     )

time: 434 us -> 545 us (1.26); the launches traced: 432 us -> 535 us
  waiting for transfers between devices: 181 us -> 220 us
  starting transfers between devices: 76.7 us -> 115 us
  local copies, waits for them, and re-layouts: 54.3 us -> 74.4 us
    all_to_all x1 -> x2, waiting for transfers between devices: 13.1 us -> 61.6 us  [the longest x1 55.2 us: grouped_projection(): back = lax.all_to_all(send, 'z', 0, 0, tiled=True)]
    ppermute x11, starting transfers between devices: 62.3 us -> 93.1 us  [exclusive_scan(): got = jax.tree.map(lambda a: lax.ppermute(a, axis, pairs), inclusive)]
    ppermute x1 -> x4, waiting for transfers between devices: 23.8 us -> 7.12 us  [grouped_projection(): got = lax.ppermute(first, SEQ, pairs)]
    all_gather x1 -> x2, waiting for transfers between devices: 74.3 us -> 89.3 us  [the longest x1 89.3 us: grouped_projection(): group_rows = lax.all_gather(y_out, 'z', axis=0, tiled=True)]
    ppermute x11, waiting for transfers between devices: 64.4 us -> 53.3 us  [exclusive_scan(): got = jax.tree.map(lambda a: lax.ppermute(a, axis, pairs), inclusive)]
    reshape x0 -> x1, local copies, waits for them, and re-layouts: none -> 8.9 us  [grouped_projection(): back = back.reshape(groups, tok + reach, blocks, 128)]
    unnamed x59 -> x57, local copies, waits for them, and re-layouts: 13.4 us -> 21.6 us
    all_to_all x1 -> x2, starting transfers between devices: 8.61 us -> 14.8 us  [the longest x1 9.6 us: on_device(): got = lax.all_to_all(send, SEQ, split_axis=0, concat_axis=0, tiled=True)]
  transfers between devices with their start and end apart: 16 -> 21, of which waited for: 10 -> 12; matrix products, arithmetic and copies ran while one was open for 25% -> 22% of each run, Pallas kernels for 0% -> 0%
where the time goes in v3:
time: 545 us; the launch traced here: 535 us
  waiting for transfers between devices  220 us (40%)
  starting transfers between devices  115 us (21%)
  local copies, waits for them, and re-layouts  74.4 us (14%)
  matrix products  68.3 us (13%)
  other arithmetic  40.9 us (8%)
  between operations  15.8 us (3%)
    ppermute x11, starting transfers between devices, exclusive_scan(): got = jax.tree.map(lambda a: lax.ppermute(a, axis, pairs), inclusive)  93.1 us
    all_gather x1, waiting for transfers between devices, grouped_projection(): group_rows = lax.all_gather(y_out, 'z', axis=0, tiled=True)  89.3 us
    all_to_all x1, waiting for transfers between devices, grouped_projection(): back = lax.all_to_all(send, 'z', 0, 0, tiled=True)  55.2 us
    ppermute x11, waiting for transfers between devices, exclusive_scan(): got = jax.tree.map(lambda a: lax.ppermute(a, axis, pairs), inclusive)  53.3 us
    dot_general x1, matrix products, grouped_projection(): jnp.dot(extended, gathered_weight, preferred_element_type=jnp.float32)  23.2 us
    unnamed x57, local copies, waits for them, and re-layouts  21.6 us
    dot_general x2, matrix products, segment_summands(): intra = jnp.einsum('gkts,sgkp->tgkp', weights, xs, precision=high)  18.6 us
    dot_general x3, matrix products, inter_term(): jnp.einsum('tgn,gkpn->tgkp', cmat, state_in, precision=high)  14.1 us
  transfers between devices with their start and end apart: 21, of which 12 were waited for; matrix products, arithmetic and copies ran while one was open for 22% of the time, Pallas kernels for 0%

profile of v3, /device:TPU:1, one launch (start us, length us, event | category | flops | bytes accessed | tf_op | source)
XLA Modules:
  0.0 534.6 jit_solution(2518962501709668142)
XLA Ops:
  11.5 2.7 fusion.105
  15.8 2.0 fusion.107
  24.3 2.5 fusion.46
  26.9 4.4 collective-permute-start
  31.2 21.8 %collective-permute-done = f32[2,16,64,128]{3,2,1,0:T(8,128)S(1)} collective-permute-done((f32[2,16,64,128]{3,2,1,0:T(8,128)S(1)}, f32[2,16,64,128]{3,2,1,0:T(8,128)S(1)}, u32[]{:S(2)}, u32[]{:S(2)}) %collective-permute-start) | collective-permute-done | bytes 1048608 | tf_op jit(solution)/shard_map/ppermute | solution.py:70
  53.2 6.1 %collective-permute-start.1 = (f32[2,16,64,128]{3,2,1,0:T(8,128)S(1)}, f32[2,16,64,128]{3,2,1,0:T(8,128)S(1)}, u32[]{:S(2)}, u32[]{:S(2)}) collective-permute-start(f32[2,16,64,128]{3,2,1,0:T(8,128)S(1)} %multiply_add_fusion.4), channel_id=1, source_target_pairs={{0,4},{2,6},{4,8},{6,10},{8,12},{10,14},{12,16},{14,18},{16,20},{1... | collective-permute-start | bytes 3145736 | tf_op jit(solution)/shard_map/ppermute | solution.py:70
  59.3 6.5 %collective-permute-start.2 = (f32[2,16]{1,0:T(2,128)S(1)}, f32[2,16]{1,0:T(2,128)S(1)}, u32[]{:S(2)}, u32[]{:S(2)}) collective-permute-start(f32[2,16]{1,0:T(2,128)S(1)} %get-tuple-element.58), channel_id=1, source_target_pairs={{0,2},{2,4},{4,6},{6,8},{8,10},{10,12},{12,14},{14,16},{16,18},{18... | collective-permute-start | bytes 392 | tf_op jit(solution)/shard_map/ppermute | solution.py:70
  65.8 14.4 %collective-permute-done.2 = f32[2,16]{1,0:T(2,128)S(1)} collective-permute-done((f32[2,16]{1,0:T(2,128)S(1)}, f32[2,16]{1,0:T(2,128)S(1)}, u32[]{:S(2)}, u32[]{:S(2)}) %collective-permute-start.2) | collective-permute-done | bytes 160 | tf_op jit(solution)/shard_map/ppermute | solution.py:70
  80.9 29.2 %collective-permute-start.3 = (f32[2,16,64,128]{3,2,1,0:T(8,128)S(1)}, f32[2,16,64,128]{3,2,1,0:T(8,128)}, u32[]{:S(2)}, u32[]{:S(2)}) collective-permute-start(f32[2,16,64,128]{3,2,1,0:T(8,128)S(1)} %multiply_add_fusion.3), channel_id=1, source_target_pairs={{0,8},{2,10},{4,12},{6,14},{8,16},{10,18},{12,20},{14,22},{16,24},... | collective-permute-start | bytes 3145736 | tf_op jit(solution)/shard_map/ppermute | solution.py:70
  113.3 5.1 reduce-window.26
  127.0 2.4 multiply_add_fusion.2
  129.3 22.0 %collective-permute-start.5 = (f32[2,16,64,128]{3,2,1,0:T(8,128)}, f32[2,16,64,128]{3,2,1,0:T(8,128)S(1)}, u32[]{:S(2)}, u32[]{:S(2)}) collective-permute-start(f32[2,16,64,128]{3,2,1,0:T(8,128)} %multiply_add_fusion.2), channel_id=1, source_target_pairs={{0,16},{2,18},{4,20},{6,22},{8,24},{10,26},{12,28},{14,30},{16,32}... | collective-permute-start | bytes 3145736 | tf_op jit(solution)/shard_map/ppermute | solution.py:70
  152.4 2.3 fusion.75
  154.7 2.3 fusion.113
  157.0 2.2 collective-permute-start.6
  159.3 4.2 copy.165
  164.2 7.7 %collective-permute-done.6 = f32[2,16]{1,0:T(2,128)S(1)} collective-permute-done((f32[2,16]{1,0:T(2,128)S(1)}, f32[2,16]{1,0:T(2,128)S(1)}, u32[]{:S(2)}, u32[]{:S(2)}) %collective-permute-start.6) | collective-permute-done | bytes 160 | tf_op jit(solution)/shard_map/ppermute | solution.py:70
  171.9 2.7 multiply_add_fusion.1
  174.7 10.4 %collective-permute-start.7 = (f32[2,16,64,128]{3,2,1,0:T(8,128)}, f32[2,16,64,128]{3,2,1,0:T(8,128)}, u32[]{:S(2)}, u32[]{:S(2)}) collective-permute-start(f32[2,16,64,128]{3,2,1,0:T(8,128)} %multiply_add_fusion.1), channel_id=1, source_target_pairs={{0,32},{2,34},{4,36},{6,38},{8,40},{10,42},{12,44},{14,46},{16,48}... | collective-permute-start | bytes 3145736 | tf_op jit(solution)/shard_map/ppermute | solution.py:70
  185.2 9.3 %fusion.31 = f32[256,2,16,64]{0,3,2,1:T(8,128)} fusion(f32[2,16,64,256]{3,2,1,0:T(8,128)} %fusion.113, bf16[256,2,16,64]{0,3,2,1:T(8,128)(2,1)} %bitcast.175, f32[2,16,256]{2,1,0:T(8,128)S(1)} %bitcast.194, f32[2,16,256]{2,1,0:T(8,128)S(1)} %copy-done.18, f32[2,256,256]{2,1,0:T(8,128)} %fusion.112, pred[256,256]{1,0:T(8,128)(4,1)S(1)} %iota_compare_fusion.2, ...), kind=kOutput, calls=%fused_computation.42 | convolution fusion | flops 1622147072 | bytes 5931008 | tf_op jit(solution)/shard_map/gkts,sgkp->tgkp/dot_general | solution.py:27
  196.1 2.9 copy.167
  199.6 4.1 collective-permute-done.7
  203.7 2.7 multiply_add_fusion
  206.4 6.5 %collective-permute-start.9 = (f32[2,16,64,128]{3,2,1,0:T(8,128)}, f32[2,16,64,128]{3,2,1,0:T(8,128)}, u32[]{:S(2)}, u32[]{:S(2)}) collective-permute-start(f32[2,16,64,128]{3,2,1,0:T(8,128)} %multiply_add_fusion), channel_id=1, source_target_pairs={{0,64},{2,66},{4,68},{6,70},{8,72},{10,74},{12,76},{14,78},{16,80}... | collective-permute-start | bytes 3145736 | tf_op jit(solution)/shard_map/ppermute | solution.py:70
  212.9 9.3 %fusion.32 = f32[256,2,16,64]{0,3,2,1:T(8,128)} fusion(f32[2,16,64,256]{3,2,1,0:T(8,128)} %fusion.75, bf16[256,2,16,64]{0,3,2,1:T(8,128)(2,1)} %bitcast.173, f32[2,16,256]{2,1,0:T(8,128)S(1)} %bitcast.192, f32[2,16,256]{2,1,0:T(8,128)S(1)} %copy-done.17, f32[2,256,256]{2,1,0:T(8,128)} %fusion.111, pred[256,256]{1,0:T(8,128)(4,1)} %copy-done.16, ...), kind=kOutput, calls=%fused_computation.44 | convolution fusion | flops 1622147072 | bytes 5931008 | tf_op jit(solution)/shard_map/gkts,sgkp->tgkp/dot_general | solution.py:27
  222.3 2.9 collective-permute-start.10
  225.9 4.8 collective-permute-done.10
  230.8 9.5 %multiply_reduce_fusion = (f32[512,2]{0,1:T(2,128)S(1)}, f32[512,2,16,64]{0,3,2,1:T(8,128)}) fusion(f32[512,2048]{0,1:T(8,128)} %copy.167, f32[512,2,16,64]{0,3,2,1:T(8,128)} %bitcast.170, f32[2,16]{1,0:T(2,128)S(1)} %mul.264, bf16[512,2,128,1]{2,1,0,3:T(2,128)(2,1)S(1)} %bitcast.184, f32[2,16,64,128]{3,2,1,0:T(8,128)} %copy-done.4, ...), kind=kOutput, calls=%fused_computation.28 | convolution fusion | flops 1625816064 | bytes 23401216 | tf_op jit(solution)/shard_map/tgn,gkpn->tgkp/dot_general | solution.py:35
  241.6 4.0 copy.201
  245.6 5.4 %copy.166 = f32[512,2048]{1,0:T(8,128)} copy(f32[512,2048]{0,1:T(8,128)} %bitcast.171) | data formatting | bytes 8388608 | tf_op jit(solution)/shard_map/reshape | solution.py:150
  251.0 6.4 %multiply_convert_fusion = bf16[512,2048]{1,0:T(8,128)(2,1)} fusion(f32[512,2048]{1,0:T(8,128)} %bitcast.169, f32[512,2048]{1,0:T(8,128)} %copy.166, f32[2048]{0:T(1024)S(1)} %copy-done.20, bf16[512,2048]{1,0:T(8,128)(2,1)S(1)} %copy-done.2), kind=kLoop, calls=%fused_computation.27 | loop fusion | flops 9437184 | bytes 12591104 | tf_op jit(solution)/shard_map/convert_element_type | solution.py:156
  262.9 7.1 %collective-permute-done.11 = bf16[128,2048]{1,0:T(8,128)(2,1)S(1)} collective-permute-done((bf16[128,2048]{1,0:T(8,128)(2,1)}, bf16[128,2048]{1,0:T(8,128)(2,1)S(1)}, u32[]{:S(2)}, u32[]{:S(2)}) %collective-permute-start.11) | collective-permute-done | bytes 524320 | tf_op jit(solution)/shard_map/ppermute | solution.py:100
  270.9 89.3 %all-gather.3.cloned.1.call-done = bf16[2048,2048]{1,0:T(8,128)(2,1)} async-done(((bf16[512,2048]{1,0:T(8,128)(2,1)}), bf16[2048,2048]{1,0:T(8,128)(2,1)}) %all-gather.3.cloned.1.call-update) | async-done | bytes 8388624 | tf_op jit(solution)/shard_map/all_gather | solution.py:95
  360.2 23.2 %convolution_convert_fusion = bf16[2176,2048]{1,0:T(8,128)(2,1)S(1)} fusion(bf16[2048,2048]{1,0:T(8,128)(2,1)} %all-gather.5.cloned.1.call-done, bf16[128,2048]{1,0:T(8,128)(2,1)} %add_add_fusion, bf16[2048,2048]{1,0:T(8,128)(2,1)} %all-gather.3.cloned.1.call-done), kind=kOutput, calls=%fused_computation.1 | convolution fusion | flops 18275893248 | bytes 26214400 | tf_op jit(solution)/shard_map/dot_general | solution.py:103
  383.5 2.9 constant_dynamic-slice_fusion
  388.9 7.5 %collective-permute-done.15 = bf16[2176,1024]{1,0:T(8,128)(2,1)} collective-permute-done((bf16[2176,1024]{1,0:T(8,128)(2,1)}, bf16[2176,1024]{1,0:T(8,128)(2,1)}, u32[]{:S(2)}, u32[]{:S(2)}) %collective-permute-start.15) | collective-permute-done | bytes 4456480 | tf_op jit(solution)/shard_map/ppermute | solution.py:86
  396.4 5.9 %add_convert_fusion = bf16[2176,1024]{1,0:T(8,128)(2,1)S(1)} fusion(bf16[2176,1024]{1,0:T(8,128)(2,1)} %collective-permute-done.15, bf16[2176,2048]{1,0:T(8,128)(2,1)} %copy-done.1, s32[]{:T(128)S(6)} %select_n.53), kind=kLoop, calls=%fused_computation.5 | loop fusion | flops 8912896 | bytes 13369348 | tf_op jit(solution)/shard_map/convert_element_type | solution.py:87
  403.3 2.9 pad_maximum_fusion
  406.2 5.2 all-to-all-start
  416.1 55.2 %all-to-all-done = bf16[4,640,1024]{2,1,0:T(8,128)(2,1)} async-done(((bf16[4,640,1024]{2,1,0:T(8,128)(2,1)}), bf16[4,640,1024]{2,1,0:T(8,128)(2,1)}, u32[]{:S(2)}, u32[]{:S(2)}) %all-to-all-start) | async-done | bytes 5242912 | tf_op jit(solution)/shard_map/all_to_all | solution.py:106
  471.3 6.2 %copy.202 = bf16[320,8,8,128]{3,2,1,0:T(8,128)(2,1)} copy(bf16[320,8,8,128]{3,1,2,0:T(8,128)(2,1)} %bitcast.85) | data formatting | bytes 10485760
  477.5 8.9 %copy.169 = bf16[4,640,8,128]{1,3,0,2:T(8,128)(2,1)} copy(bf16[4,640,8,128]{3,2,1,0:T(8,128)(2,1)} %bitcast.164) | data formatting | bytes 10485760 | tf_op jit(solution)/shard_map/reshape | solution.py:108
  486.4 4.2 fusion.17
  493.2 9.6 %all-to-all-start.1 = ((bf16[64,2,4224]{2,1,0:T(2,128)(2,1)}), bf16[64,2,4224]{2,1,0:T(2,128)(2,1)S(1)}, u32[]{:S(2)}, u32[]{:S(2)}) async-start(bf16[64,2,4224]{2,1,0:T(2,128)(2,1)} %reshape.283), calls=%async_computation.1 | async-start | bytes 2162688 | tf_op jit(solution)/shard_map/all_to_all | solution.py:184
  502.8 4.7 slice.202
  507.5 6.3 %copy.171 = bf16[512,4096]{1,0:T(8,128)(2,1)} copy(bf16[512,4096]{0,1:T(8,128)(2,1)} %bitcast.168) | data formatting | bytes 8388608
  513.8 6.4 %all-to-all-done.1 = bf16[64,2,4224]{2,1,0:T(2,128)(2,1)S(1)} async-done(((bf16[64,2,4224]{2,1,0:T(2,128)(2,1)}), bf16[64,2,4224]{2,1,0:T(2,128)(2,1)S(1)}, u32[]{:S(2)}, u32[]{:S(2)}) %all-to-all-start.1) | async-done | bytes 1081376 | tf_op jit(solution)/shard_map/all_to_all | solution.py:184
  521.3 2.7 collective-permute-start.16
  (154 shorter events, 51.8 us)
Async XLA Ops:
  7.2 513.6 %copy-start = (bf16[1,4096,128]{2,1,0:T(8,128)(2,1)S(1)}, bf16[1,4096,128]{2,1,0:T(8,128)(2,1)}, u32[]{:S(2)}) copy-start(bf16[1,4096,128]{2,1,0:T(8,128)(2,1)} %param.27) | copy-start | bytes 3145732
  7.2 263.7 %all-gather.5.cloned.1.call-start = ((), (), s32[]{:S(2)}) async-start(), calls=%async_computation.3 | async-start | bytes 8912896 | tf_op jit(solution)/shard_map/all_gather | solution.py:94
  7.9 352.3 %all-gather.3.cloned.1.call-start = ((), (), s32[]{:S(2)}) async-start(), calls=%async_computation.2 | async-start | bytes 10485760 | tf_op jit(solution)/shard_map/all_gather | solution.py:95
  11.5 10.2 %copy-start.14 = (f32[512,32]{0,1:T(8,128)S(1)}, f32[512,32]{0,1:T(8,128)}, u32[]{:S(2)}) copy-start(f32[512,32]{0,1:T(8,128)} %param.22) | copy-start | bytes 196612
  15.8 11.1 %copy-start.3 = (bf16[256,2048]{0,1:T(8,128)(2,1)}, bf16[256,2048]{0,1:T(8,128)(2,1)S(1)}, u32[]{:S(2)}) copy-start(bf16[256,2048]{0,1:T(8,128)(2,1)S(1)} %copy.146) | copy-start | bytes 3145732
  21.7 1.4 copy-start.10
  21.7 2.6 copy-start.12
  24.3 85.8 %copy-start.7 = (bf16[512,256]{1,0:T(8,128)(2,1)S(1)}, bf16[512,256]{1,0:T(8,128)(2,1)}, u32[]{:S(2)}) copy-start(bf16[512,256]{1,0:T(8,128)(2,1)} %param.21) | copy-start | bytes 786436
  26.9 26.2 %collective-permute-start = (f32[2,16,64,128]{3,2,1,0:T(8,128)S(1)}, f32[2,16,64,128]{3,2,1,0:T(8,128)S(1)}, u32[]{:S(2)}, u32[]{:S(2)}) collective-permute-start(f32[2,16,64,128]{3,2,1,0:T(8,128)S(1)} %fusion.46), channel_id=1, source_target_pairs={{0,2},{2,4},{4,6},{6,8},{8,10},{10,12},{12,14},{14,16},{16,18},{18... | collective-permute-start | bytes 3145736 | tf_op jit(solution)/shard_map/ppermute | solution.py:70
  53.0 57.8 %copy-start.4 = (f32[2,16,64,128]{3,2,1,0:T(8,128)}, f32[2,16,64,128]{3,2,1,0:T(8,128)S(1)}, u32[]{:S(2)}) copy-start(f32[2,16,64,128]{3,2,1,0:T(8,128)S(1)} %collective-permute-done) | copy-start | bytes 3145732
  53.2 27.6 %collective-permute-start.1 = (f32[2,16,64,128]{3,2,1,0:T(8,128)S(1)}, f32[2,16,64,128]{3,2,1,0:T(8,128)S(1)}, u32[]{:S(2)}, u32[]{:S(2)}) collective-permute-start(f32[2,16,64,128]{3,2,1,0:T(8,128)S(1)} %multiply_add_fusion.4), channel_id=1, source_target_pairs={{0,4},{2,6},{4,8},{6,10},{8,12},{10,14},{12,16},{14,18},{16,20},{1... | collective-permute-start | bytes 3145736 | tf_op jit(solution)/shard_map/ppermute | solution.py:70
  59.3 20.9 %collective-permute-start.2 = (f32[2,16]{1,0:T(2,128)S(1)}, f32[2,16]{1,0:T(2,128)S(1)}, u32[]{:S(2)}, u32[]{:S(2)}) collective-permute-start(f32[2,16]{1,0:T(2,128)S(1)} %get-tuple-element.58), channel_id=1, source_target_pairs={{0,2},{2,4},{4,6},{6,8},{8,10},{10,12},{12,14},{14,16},{16,18},{18... | collective-permute-start | bytes 392 | tf_op jit(solution)/shard_map/ppermute | solution.py:70
  80.8 30.1 %copy-start.5 = (f32[2,16,64,128]{3,2,1,0:T(8,128)}, f32[2,16,64,128]{3,2,1,0:T(8,128)S(1)}, u32[]{:S(2)}) copy-start(f32[2,16,64,128]{3,2,1,0:T(8,128)S(1)} %collective-permute-done.1) | copy-start | bytes 3145732
  80.9 46.0 %collective-permute-start.3 = (f32[2,16,64,128]{3,2,1,0:T(8,128)S(1)}, f32[2,16,64,128]{3,2,1,0:T(8,128)}, u32[]{:S(2)}, u32[]{:S(2)}) collective-permute-start(f32[2,16,64,128]{3,2,1,0:T(8,128)S(1)} %multiply_add_fusion.3), channel_id=1, source_target_pairs={{0,8},{2,10},{4,12},{6,14},{8,16},{10,18},{12,20},{14,22},{16,24},... | collective-permute-start | bytes 3145736 | tf_op jit(solution)/shard_map/ppermute | solution.py:70
  123.6 2.3 collective-permute-start.4
  129.3 42.6 %collective-permute-start.5 = (f32[2,16,64,128]{3,2,1,0:T(8,128)}, f32[2,16,64,128]{3,2,1,0:T(8,128)S(1)}, u32[]{:S(2)}, u32[]{:S(2)}) collective-permute-start(f32[2,16,64,128]{3,2,1,0:T(8,128)} %multiply_add_fusion.2), channel_id=1, source_target_pairs={{0,16},{2,18},{4,20},{6,22},{8,24},{10,26},{12,28},{14,30},{16,32}... | collective-permute-start | bytes 3145736 | tf_op jit(solution)/shard_map/ppermute | solution.py:70
  154.7 8.7 %copy-start.8 = (bf16[512,256]{1,0:T(8,128)(2,1)S(1)}, bf16[512,256]{1,0:T(8,128)(2,1)}, u32[]{:S(2)}) copy-start(bf16[512,256]{1,0:T(8,128)(2,1)} %param.21) | copy-start | bytes 786436
  157.0 28.1 %copy-start.13 = (f32[256,32]{0,1:T(8,128)S(1)}, f32[256,32]{0,1:T(8,128)}, u32[]{:S(2)}) copy-start(f32[256,32]{0,1:T(8,128)} %copy-done.12) | copy-start | bytes 98308
  157.0 28.1 %copy-start.18 = (f32[2,16,256]{2,1,0:T(8,128)S(1)}, f32[2,16,256]{2,1,0:T(8,128)}, u32[]{:S(2)}) copy-start(f32[2,16,256]{2,1,0:T(8,128)} %get-tuple-element.76) | copy-start | bytes 98308
  157.0 28.1 %copy-start.19 = (f32[256,2,16]{0,2,1:T(8,128)S(1)}, f32[256,2,16]{0,2,1:T(8,128)}, u32[]{:S(2)}) copy-start(f32[256,2,16]{0,2,1:T(8,128)} %get-tuple-element.74) | copy-start | bytes 98308
  157.0 14.9 %collective-permute-start.6 = (f32[2,16]{1,0:T(2,128)S(1)}, f32[2,16]{1,0:T(2,128)S(1)}, u32[]{:S(2)}, u32[]{:S(2)}) collective-permute-start(f32[2,16]{1,0:T(2,128)S(1)} %get-tuple-element.54), channel_id=1, source_target_pairs={{0,8},{2,10},{4,12},{6,14},{8,16},{10,18},{12,20},{14,22},{16,24},... | collective-permute-start | bytes 392 | tf_op jit(solution)/shard_map/ppermute | solution.py:70
  171.9 13.2 %copy-start.6 = (f32[2,16,64,128]{3,2,1,0:T(8,128)}, f32[2,16,64,128]{3,2,1,0:T(8,128)S(1)}, u32[]{:S(2)}) copy-start(f32[2,16,64,128]{3,2,1,0:T(8,128)S(1)} %collective-permute-done.5) | copy-start | bytes 3145732
  174.7 29.0 %collective-permute-start.7 = (f32[2,16,64,128]{3,2,1,0:T(8,128)}, f32[2,16,64,128]{3,2,1,0:T(8,128)}, u32[]{:S(2)}, u32[]{:S(2)}) collective-permute-start(f32[2,16,64,128]{3,2,1,0:T(8,128)} %multiply_add_fusion.1), channel_id=1, source_target_pairs={{0,32},{2,34},{4,36},{6,38},{8,40},{10,42},{12,44},{14,46},{16,48}... | collective-permute-start | bytes 3145736 | tf_op jit(solution)/shard_map/ppermute | solution.py:70
  185.1 9.3 %copy-start.16 = (pred[256,256]{1,0:T(8,128)(4,1)}, pred[256,256]{1,0:T(8,128)(4,1)S(1)}, u32[]{:S(2)}) copy-start(pred[256,256]{1,0:T(8,128)(4,1)S(1)} %iota_compare_fusion.2) | copy-start | bytes 196612
  185.2 10.9 %copy-start.2 = (bf16[512,2048]{1,0:T(8,128)(2,1)S(1)}, bf16[512,2048]{1,0:T(8,128)(2,1)}, u32[]{:S(2)}) copy-start(bf16[512,2048]{1,0:T(8,128)(2,1)} %param.19) | copy-start | bytes 6291460
  194.5 18.5 %copy-start.11 = (f32[256,32]{0,1:T(8,128)S(1)}, f32[256,32]{0,1:T(8,128)}, u32[]{:S(2)}) copy-start(f32[256,32]{0,1:T(8,128)} %copy-done.10) | copy-start | bytes 98308
  194.5 18.5 %copy-start.17 = (f32[2,16,256]{2,1,0:T(8,128)S(1)}, f32[2,16,256]{2,1,0:T(8,128)}, u32[]{:S(2)}) copy-start(f32[2,16,256]{2,1,0:T(8,128)} %get-tuple-element.79) | copy-start | bytes 98308
  194.5 4.6 collective-permute-start.8
  206.4 24.4 %collective-permute-start.9 = (f32[2,16,64,128]{3,2,1,0:T(8,128)}, f32[2,16,64,128]{3,2,1,0:T(8,128)}, u32[]{:S(2)}, u32[]{:S(2)}) collective-permute-start(f32[2,16,64,128]{3,2,1,0:T(8,128)} %multiply_add_fusion), channel_id=1, source_target_pairs={{0,64},{2,66},{4,68},{6,70},{8,72},{10,74},{12,76},{14,78},{16,80}... | collective-permute-start | bytes 3145736 | tf_op jit(solution)/shard_map/ppermute | solution.py:70
  212.9 17.8 %copy-start.9 = (bf16[512,2,128]{2,1,0:T(2,128)(2,1)S(1)}, bf16[512,2,128]{2,1,0:T(2,128)(2,1)}, u32[]{:S(2)}) copy-start(bf16[512,2,128]{2,1,0:T(2,128)(2,1)} %reshape.273) | copy-start | bytes 786436
  212.9 17.8 %copy-start.15 = (f32[512,2,16]{0,2,1:T(8,128)S(1)}, f32[512,2,16]{0,2,1:T(8,128)}, u32[]{:S(2)}) copy-start(f32[512,2,16]{0,2,1:T(8,128)} %bitcast_bitcast_fusion) | copy-start | bytes 196612
  222.3 8.4 %collective-permute-start.10 = (f32[2,16]{1,0:T(2,128)}, f32[2,16]{1,0:T(2,128)S(1)}, u32[]{:S(2)}, u32[]{:S(2)}) collective-permute-start(f32[2,16]{1,0:T(2,128)} %get-tuple-element.50), channel_id=1, source_target_pairs={{0,32},{2,34},{4,36},{6,38},{8,40},{10,42},{12,44},{14,46},{16,48}... | collective-permute-start | bytes 392 | tf_op jit(solution)/shard_map/ppermute | solution.py:70
  245.6 5.4 %copy-start.20 = (f32[2048]{0:T(1024)S(1)}, f32[2048]{0:T(1024)}, u32[]{:S(2)}) copy-start(f32[2048]{0:T(1024)} %param.25) | copy-start | bytes 24580
  259.3 10.7 %collective-permute-start.11 = (bf16[128,2048]{1,0:T(8,128)(2,1)}, bf16[128,2048]{1,0:T(8,128)(2,1)S(1)}, u32[]{:S(2)}, u32[]{:S(2)}) collective-permute-start(bf16[128,2048]{1,0:T(8,128)(2,1)} %slice.197), channel_id=1, source_target_pairs={{8,0},{16,8},{24,16},{32,24},{40,32},{48,40},{56,48},{64,56},{72,6... | collective-permute-start | bytes 1572872 | tf_op jit(solution)/shard_map/ppermute | solution.py:100
  260.6 9.4 %collective-permute-start.12 = (bf16[128,2048]{1,0:T(8,128)(2,1)}, bf16[128,2048]{1,0:T(8,128)(2,1)S(1)}, u32[]{:S(2)}, u32[]{:S(2)}) collective-permute-start(bf16[128,2048]{1,0:T(8,128)(2,1)} %slice.197), channel_id=1, source_target_pairs={{8,2},{16,10},{24,18},{32,26},{40,34},{48,42},{56,50},{64,58},{72,... | collective-permute-start | bytes 1572872 | tf_op jit(solution)/shard_map/ppermute | solution.py:100
  261.3 8.7 %collective-permute-start.13 = (bf16[128,2048]{1,0:T(8,128)(2,1)}, bf16[128,2048]{1,0:T(8,128)(2,1)S(1)}, u32[]{:S(2)}, u32[]{:S(2)}) collective-permute-start(bf16[128,2048]{1,0:T(8,128)(2,1)} %slice.197), channel_id=1, source_target_pairs={{8,4},{16,12},{24,20},{32,28},{40,36},{48,44},{56,52},{64,60},{72,... | collective-permute-start | bytes 1572872 | tf_op jit(solution)/shard_map/ppermute | solution.py:100
  262.0 8.0 %collective-permute-start.14 = (bf16[128,2048]{1,0:T(8,128)(2,1)}, bf16[128,2048]{1,0:T(8,128)(2,1)S(1)}, u32[]{:S(2)}, u32[]{:S(2)}) collective-permute-start(bf16[128,2048]{1,0:T(8,128)(2,1)} %slice.197), channel_id=1, source_target_pairs={{8,6},{16,14},{24,22},{32,30},{40,38},{48,46},{56,54},{64,62},{72,... | collective-permute-start | bytes 1572872 | tf_op jit(solution)/shard_map/ppermute | solution.py:100
  383.4 4.8 copy-start.1
  388.2 8.1 %collective-permute-start.15 = (bf16[2176,1024]{1,0:T(8,128)(2,1)}, bf16[2176,1024]{1,0:T(8,128)(2,1)}, u32[]{:S(2)}, u32[]{:S(2)}) collective-permute-start(bf16[2176,1024]{1,0:T(8,128)(2,1)} %constant_dynamic-slice_fusion), channel_id=1, source_target_pairs={{0,1},{1,0},{2,3},{3,2},{4,5},{5,4},{6,7},{7,6},{8,9},{9,8},{10,11... | collective-permute-start | bytes 13369352 | tf_op jit(solution)/shard_map/ppermute | solution.py:86
  406.2 6.5 %copy-start.23 = (s32[64]{0:T(128)S(1)}, s32[64]{0:T(128)}, u32[]{:S(2)}) copy-start(s32[64]{0:T(128)} %param.31) | copy-start | bytes 772
  406.2 8.9 %copy-start.24 = (s32[64,1]{0,1:T(1,128)S(1)}, s32[64,1]{0,1:T(1,128)}, u32[]{:S(2)}) copy-start(s32[64,1]{0,1:T(1,128)} %param.30) | copy-start | bytes 772
  406.2 9.8 %copy-start.21 = (s32[64]{0:T(128)S(1)}, s32[64]{0:T(128)}, u32[]{:S(2)}) copy-start(s32[64]{0:T(128)} %param.29) | copy-start | bytes 772
  406.2 9.8 %copy-start.22 = (s32[64]{0:T(128)S(1)}, s32[64]{0:T(128)}, u32[]{:S(2)}) copy-start(s32[64]{0:T(128)} %param.28) | copy-start | bytes 772
  406.2 65.0 %all-to-all-start = ((bf16[4,640,1024]{2,1,0:T(8,128)(2,1)}), bf16[4,640,1024]{2,1,0:T(8,128)(2,1)}, u32[]{:S(2)}, u32[]{:S(2)}) async-start(bf16[4,640,1024]{2,1,0:T(8,128)(2,1)} %pad_maximum_fusion), calls=%async_computation | async-start | bytes 10485760 | tf_op jit(solution)/shard_map/all_to_all | solution.py:106
  493.2 27.0 %all-to-all-start.1 = ((bf16[64,2,4224]{2,1,0:T(2,128)(2,1)}), bf16[64,2,4224]{2,1,0:T(2,128)(2,1)S(1)}, u32[]{:S(2)}, u32[]{:S(2)}) async-start(bf16[64,2,4224]{2,1,0:T(2,128)(2,1)} %reshape.283), calls=%async_computation.1 | async-start | bytes 2162688 | tf_op jit(solution)/shard_map/all_to_all | solution.py:184
  521.3 3.6 collective-permute-start.16
Sparse Core Ops, SparseCore 0:
  10.1 97.3 all-gather.4
  257.5 102.6 all-gather.2

commit v4 on v3

--- a/solution.py
+++ b/solution.py
@@ -92,7 +92,15 @@
     groups = lax.axis_size("z")
     planes = lax.axis_size("plane")
     gathered_weight = lax.all_gather(out_weight, "plane", axis=1, tiled=True)
-    group_rows = lax.all_gather(y_out, "z", axis=0, tiled=True)
+    me = lax.axis_index("z")
+
+    def around(value, shift):
+        pairs = [(p * groups + z, p * groups + (z + shift) % groups) for p in range(planes) for z in range(groups)]
+        return lax.ppermute(value, SEQ, pairs)
+
+    received = jnp.stack([y_out] + [around(y_out, s) for s in range(1, groups)])
+    order = (me - jnp.arange(groups)) % groups
+    group_rows = jnp.take(received, order, axis=0).reshape(groups * tok, -1)
     first = y_out[:reach]
     extra = None
     for target in range(groups):
@@ -102,8 +110,12 @@
     extended = jnp.concatenate([group_rows, extra], axis=0)
     part = jnp.dot(extended, gathered_weight, preferred_element_type=jnp.float32)
     summed = head_sum(part.astype(jnp.bfloat16), "head")
-    send = jnp.stack([summed[z * tok : z * tok + tok + reach] for z in range(groups)])
-    back = lax.all_to_all(send, "z", 0, 0, tiled=True)
+    chunks = [
+        around(lax.dynamic_slice_in_dim(summed, ((me + s) % groups) * tok, tok + reach, 0), s)
+        for s in range(1, groups)
+    ]
+    own = lax.dynamic_slice_in_dim(summed, me * tok, tok + reach, 0)
+    back = jnp.take(jnp.stack([own] + chunks), order, axis=0)
     blocks = summed.shape[1] // 128
     back = back.reshape(groups, tok + reach, blocks, 128)
     return jnp.transpose(back, (1, 2, 0, 3)).reshape(tok + reach, groups * blocks * 128)

time: 545 us -> 589 us (1.081)
  other arithmetic: 40.9 us -> 68.2 us
  local copies, waits for them, and re-layouts: 74.4 us -> 90.9 us
  starting transfers between devices: 115 us -> 122 us
    ppermute x0 -> x6, waiting for transfers between devices: none -> 142 us  [around(): return lax.ppermute(value, SEQ, pairs)]
    all_gather x1 -> x0, waiting for transfers between devices: 89.3 us -> none  [grouped_projection(): group_rows = lax.all_gather(y_out, 'z', axis=0, tiled=True)]
    all_to_all x1 -> x0, waiting for transfers between devices: 55.2 us -> none  [grouped_projection(): back = lax.all_to_all(send, 'z', 0, 0, tiled=True)]
    gather x0 -> x5, local copies, waits for them, and re-layouts: none -> 28.4 us  [the longest x2 14.5 us: grouped_projection(): back = jnp.take(jnp.stack([own] + chunks), order, axis=0)]
    select_n x0 -> x3, other arithmetic: none -> 10.6 us  [the longest x1 7.5 us: grouped_projection(): group_rows = jnp.take(received, order, axis=0).reshape(groups * tok, -1)]
    ppermute x0 -> x6, starting transfers between devices: none -> 9.33 us  [around(): return lax.ppermute(value, SEQ, pairs)]
    reshape x1 -> x0, local copies, waits for them, and re-layouts: 8.9 us -> none  [grouped_projection(): back = back.reshape(groups, tok + reach, blocks, 128)]
    unnamed x0 -> x1, other arithmetic: none -> 8.17 us
  transfers between devices with their start and end apart: 21 -> 25, of which waited for: 12 -> 14; matrix products, arithmetic and copies ran while one was open for 22% -> 27% of each run, Pallas kernels for 0% -> 0%
where the time goes in v4:
time: 589 us; the launch traced here: 579 us
  waiting for transfers between devices  216 us (37%)
  starting transfers between devices  122 us (21%)
  local copies, waits for them, and re-layouts  90.9 us (15%)
  other arithmetic  68.2 us (12%)
  matrix products  66.1 us (11%)
  between operations  15.6 us (3%)
    ppermute x6, waiting for transfers between devices, around(): return lax.ppermute(value, SEQ, pairs)  142 us
    ppermute x11, starting transfers between devices, exclusive_scan(): got = jax.tree.map(lambda a: lax.ppermute(a, axis, pairs), inclusive)  89.2 us
    ppermute x11, waiting for transfers between devices, exclusive_scan(): got = jax.tree.map(lambda a: lax.ppermute(a, axis, pairs), inclusive)  56.3 us
    dot_general x1, matrix products, grouped_projection(): jnp.dot(extended, gathered_weight, preferred_element_type=jnp.float32)  23.3 us
    unnamed x65, local copies, waits for them, and re-layouts  21.6 us
    dot_general x2, matrix products, segment_summands(): intra = jnp.einsum('gkts,sgkp->tgkp', weights, xs, precision=high)  18.7 us
    gather x2, local copies, waits for them, and re-layouts, grouped_projection(): back = jnp.take(jnp.stack([own] + chunks), order, axis=0)  14.5 us
    gather x3, local copies, waits for them, and re-layouts, grouped_projection(): group_rows = jnp.take(received, order, axis=0).reshape(groups * tok, -1)  13.8 us
  transfers between devices with their start and end apart: 25, of which 14 were waited for; matrix products, arithmetic and copies ran while one was open for 27% of the time, Pallas kernels for 0%

profile of v4, /device:TPU:1, one launch (start us, length us, event | category | flops | bytes accessed | tf_op | source)
XLA Modules:
  0.0 578.6 jit_solution(9093179972124199528)
XLA Ops:
  28.8 4.4 collective-permute-start
  33.3 21.8 %collective-permute-done = f32[2,16,64,128]{3,2,1,0:T(8,128)S(1)} collective-permute-done((f32[2,16,64,128]{3,2,1,0:T(8,128)S(1)}, f32[2,16,64,128]{3,2,1,0:T(8,128)S(1)}, u32[]{:S(2)}, u32[]{:S(2)}) %collective-permute-start) | collective-permute-done | bytes 1048608 | tf_op jit(solution)/shard_map/ppermute | solution.py:70
  55.2 6.1 %collective-permute-start.1 = (f32[2,16,64,128]{3,2,1,0:T(8,128)S(1)}, f32[2,16,64,128]{3,2,1,0:T(8,128)S(1)}, u32[]{:S(2)}, u32[]{:S(2)}) collective-permute-start(f32[2,16,64,128]{3,2,1,0:T(8,128)S(1)} %multiply_add_fusion.4), channel_id=1, source_target_pairs={{0,4},{2,6},{4,8},{6,10},{8,12},{10,14},{12,16},{14,18},{16,20},{1... | collective-permute-start | bytes 3145736 | tf_op jit(solution)/shard_map/ppermute | solution.py:70
  61.3 4.4 collective-permute-start.2
  65.7 16.5 %collective-permute-done.2 = f32[2,16]{1,0:T(2,128)S(1)} collective-permute-done((f32[2,16]{1,0:T(2,128)S(1)}, f32[2,16]{1,0:T(2,128)S(1)}, u32[]{:S(2)}, u32[]{:S(2)}) %collective-permute-start.2) | collective-permute-done | bytes 160 | tf_op jit(solution)/shard_map/ppermute | solution.py:70
  83.0 25.7 %collective-permute-start.3 = (f32[2,16,64,128]{3,2,1,0:T(8,128)S(1)}, f32[2,16,64,128]{3,2,1,0:T(8,128)}, u32[]{:S(2)}, u32[]{:S(2)}) collective-permute-start(f32[2,16,64,128]{3,2,1,0:T(8,128)S(1)} %multiply_add_fusion.3), channel_id=1, source_target_pairs={{0,8},{2,10},{4,12},{6,14},{8,16},{10,18},{12,20},{14,22},{16,24},... | collective-permute-start | bytes 3145736 | tf_op jit(solution)/shard_map/ppermute | solution.py:70
  112.0 5.1 reduce-window.26
  128.1 24.7 %collective-permute-start.5 = (f32[2,16,64,128]{3,2,1,0:T(8,128)}, f32[2,16,64,128]{3,2,1,0:T(8,128)S(1)}, u32[]{:S(2)}, u32[]{:S(2)}) collective-permute-start(f32[2,16,64,128]{3,2,1,0:T(8,128)} %multiply_add_fusion.2), channel_id=1, source_target_pairs={{0,16},{2,18},{4,20},{6,22},{8,24},{10,26},{12,28},{14,30},{16,32}... | collective-permute-start | bytes 3145736 | tf_op jit(solution)/shard_map/ppermute | solution.py:70
  159.9 4.2 copy.165
  164.8 8.6 %collective-permute-done.6 = f32[2,16]{1,0:T(2,128)S(1)} collective-permute-done((f32[2,16]{1,0:T(2,128)S(1)}, f32[2,16]{1,0:T(2,128)S(1)}, u32[]{:S(2)}, u32[]{:S(2)}) %collective-permute-start.6) | collective-permute-done | bytes 160 | tf_op jit(solution)/shard_map/ppermute | solution.py:70
  176.2 9.7 %collective-permute-start.7 = (f32[2,16,64,128]{3,2,1,0:T(8,128)}, f32[2,16,64,128]{3,2,1,0:T(8,128)}, u32[]{:S(2)}, u32[]{:S(2)}) collective-permute-start(f32[2,16,64,128]{3,2,1,0:T(8,128)} %multiply_add_fusion.1), channel_id=1, source_target_pairs={{0,32},{2,34},{4,36},{6,38},{8,40},{10,42},{12,44},{14,46},{16,48}... | collective-permute-start | bytes 3145736 | tf_op jit(solution)/shard_map/ppermute | solution.py:70
  186.1 9.3 %fusion.31 = f32[256,2,16,64]{0,3,2,1:T(8,128)} fusion(f32[2,16,64,256]{3,2,1,0:T(8,128)} %fusion.117, bf16[256,2,16,64]{0,3,2,1:T(8,128)(2,1)} %bitcast.185, f32[2,16,256]{2,1,0:T(8,128)S(1)} %bitcast.207, f32[2,16,256]{2,1,0:T(8,128)S(1)} %copy-done.20, f32[2,256,256]{2,1,0:T(8,128)} %fusion.116, pred[256,256]{1,0:T(8,128)(4,1)S(1)} %iota_compare_fusion.2, ...), kind=kOutput, calls=%fused_computation.49 | convolution fusion | flops 1622147072 | bytes 5931008 | tf_op jit(solution)/shard_map/gkts,sgkp->tgkp/dot_general | solution.py:27
  197.2 2.9 copy.167
  200.7 4.0 collective-permute-done.7
  207.4 6.9 %collective-permute-start.9 = (f32[2,16,64,128]{3,2,1,0:T(8,128)}, f32[2,16,64,128]{3,2,1,0:T(8,128)}, u32[]{:S(2)}, u32[]{:S(2)}) collective-permute-start(f32[2,16,64,128]{3,2,1,0:T(8,128)} %multiply_add_fusion), channel_id=1, source_target_pairs={{0,64},{2,66},{4,68},{6,70},{8,72},{10,74},{12,76},{14,78},{16,80}... | collective-permute-start | bytes 3145736 | tf_op jit(solution)/shard_map/ppermute | solution.py:70
  214.3 9.4 %fusion.32 = f32[256,2,16,64]{0,3,2,1:T(8,128)} fusion(f32[2,16,64,256]{3,2,1,0:T(8,128)} %fusion.75, bf16[256,2,16,64]{0,3,2,1:T(8,128)(2,1)} %bitcast.183, f32[2,16,256]{2,1,0:T(8,128)S(1)} %bitcast.205, f32[2,16,256]{2,1,0:T(8,128)S(1)} %copy-done.19, f32[2,256,256]{2,1,0:T(8,128)} %fusion.115, pred[256,256]{1,0:T(8,128)(4,1)} %copy-done.18, ...), kind=kOutput, calls=%fused_computation.51 | convolution fusion | flops 1622147072 | bytes 5931008 | tf_op jit(solution)/shard_map/gkts,sgkp->tgkp/dot_general | solution.py:27
  227.2 5.0 collective-permute-done.10
  232.2 8.9 %multiply_reduce_fusion = (f32[512,2]{0,1:T(2,128)S(1)}, f32[512,2,16,64]{0,3,2,1:T(8,128)}) fusion(f32[512,2048]{0,1:T(8,128)} %copy.167, f32[512,2,16,64]{0,3,2,1:T(8,128)} %bitcast.180, f32[2,16]{1,0:T(2,128)S(1)} %mul.276, bf16[512,2,128,1]{2,1,0,3:T(2,128)(2,1)S(1)} %bitcast.197, f32[2,16,64,128]{3,2,1,0:T(8,128)S(1)} %copy-done.5, ...), kind=kOutput, calls=%fused_computation.35 | convolution fusion | flops 1625816064 | bytes 23401216 | tf_op jit(solution)/shard_map/tgn,gkpn->tgkp/dot_general | solution.py:35
  242.4 4.0 copy.202
  246.4 5.5 copy.166
  251.9 5.7 multiply_convert_fusion
  264.6 7.7 %collective-permute-done.14 = bf16[128,2048]{1,0:T(8,128)(2,1)} collective-permute-done((bf16[128,2048]{1,0:T(8,128)(2,1)}, bf16[128,2048]{1,0:T(8,128)(2,1)}, u32[]{:S(2)}, u32[]{:S(2)}) %collective-permute-start.14) | collective-permute-done | bytes 524320 | tf_op jit(solution)/shard_map/ppermute | solution.py:108
  277.8 42.8 %collective-permute-done.11 = bf16[512,2048]{1,0:T(8,128)(2,1)} collective-permute-done((bf16[512,2048]{1,0:T(8,128)(2,1)S(1)}, bf16[512,2048]{1,0:T(8,128)(2,1)}, u32[]{:S(2)}, u32[]{:S(2)}) %collective-permute-start.11) | collective-permute-done | bytes 2097184 | tf_op jit(solution)/shard_map/ppermute | solution.py:99
  320.6 44.9 %collective-permute-done.12 = bf16[512,2048]{1,0:T(8,128)(2,1)} collective-permute-done((bf16[512,2048]{1,0:T(8,128)(2,1)S(1)}, bf16[512,2048]{1,0:T(8,128)(2,1)}, u32[]{:S(2)}, u32[]{:S(2)}) %collective-permute-start.12) | collective-permute-done | bytes 2097184 | tf_op jit(solution)/shard_map/ppermute | solution.py:99
  365.5 3.8 pad_maximum_fusion
  369.4 3.9 fusion.108
  373.2 5.0 gather_fusion.2
  378.2 5.0 gather_fusion.3
  383.2 8.2 %pad_maximum_fusion.1 = bf16[4,512,2048]{2,1,0:T(8,128)(2,1)} fusion(bf16[4,512,1024]{2,1,0:T(8,128)(2,1)} %gather_fusion.3, bf16[4,512,1024]{2,1,0:T(8,128)(2,1)} %gather_fusion.2), kind=kLoop, calls=%fused_computation.10 | loop fusion | flops 16777216 | bytes 16777216
  391.4 7.5 %bitcast_select_fusion = bf16[2048,2048]{1,0:T(8,128)(2,1)} fusion(bf16[4,512,2048]{2,1,0:T(8,128)(2,1)} %pad_maximum_fusion.1, pred[2048]{0:T(1024)(128)(4,1)S(1)} %bitcast.209), kind=kLoop, calls=%fused_computation.11 | loop fusion | flops 4194304 | bytes 16779264 | tf_op jit(solution)/shard_map/jit(_take)/select_n | solution.py:103
  398.9 23.3 %convolution_convert_fusion = bf16[2176,2048]{1,0:T(8,128)(2,1)S(1)} fusion(bf16[2048,2048]{1,0:T(8,128)(2,1)} %all-gather.2.cloned.1.call-done, bf16[128,2048]{1,0:T(8,128)(2,1)S(1)} %copy-done.11, bf16[2048,2048]{1,0:T(8,128)(2,1)} %bitcast_select_fusion), kind=kOutput, calls=%fused_computation.4 | convolution fusion | flops 18275893248 | bytes 26214400 | tf_op jit(solution)/shard_map/dot_general | solution.py:111
  422.2 2.9 constant_dynamic-slice_fusion.3
  426.9 5.4 collective-permute-start.18
  435.8 4.0 collective-permute-done.18
  439.8 5.9 %add_convert_fusion = bf16[2176,1024]{1,0:T(8,128)(2,1)S(1)} fusion(bf16[2176,1024]{1,0:T(8,128)(2,1)} %collective-permute-done.18, bf16[2176,2048]{1,0:T(8,128)(2,1)} %copy-done.1, s32[]{:T(128)S(6)} %select_n.130), kind=kLoop, calls=%fused_computation.8 | loop fusion | flops 8912896 | bytes 13369348 | tf_op jit(solution)/shard_map/convert_element_type | solution.py:87
  446.4 3.9 collective-permute-start.20
  453.2 24.3 %collective-permute-done.19 = bf16[640,1024]{1,0:T(8,128)(2,1)S(1)} collective-permute-done((bf16[640,1024]{1,0:T(8,128)(2,1)S(1)}, bf16[640,1024]{1,0:T(8,128)(2,1)S(1)}, u32[]{:S(2)}, u32[]{:S(2)}) %collective-permute-start.19) | collective-permute-done | bytes 1310752 | tf_op jit(solution)/shard_map/ppermute | solution.py:99
  477.5 29.5 %collective-permute-done.20 = bf16[640,1024]{1,0:T(8,128)(2,1)S(1)} collective-permute-done((bf16[640,1024]{1,0:T(8,128)(2,1)S(1)}, bf16[640,1024]{1,0:T(8,128)(2,1)S(1)}, u32[]{:S(2)}, u32[]{:S(2)}) %collective-permute-start.20) | collective-permute-done | bytes 1310752 | tf_op jit(solution)/shard_map/ppermute | solution.py:99
  507.1 2.9 pad_maximum_fusion.2
  509.9 5.7 gather_fusion
  515.6 6.2 %copy.203 = bf16[320,8,8,128]{3,2,1,0:T(8,128)(2,1)} copy(bf16[320,8,8,128]{3,1,2,0:T(8,128)(2,1)} %bitcast.173) | data formatting | bytes 10485760
  521.8 8.9 %copy.169 = bf16[4,640,8,128]{1,3,0,2:T(8,128)(2,1)} copy(bf16[4,640,8,128]{3,2,1,0:T(8,128)(2,1)} %bitcast.174) | data formatting | bytes 10485760 | tf_op jit(solution)/shard_map/jit(_take)/gather | solution.py:118
  530.7 3.1 broadcast_select_fusion
  538.1 8.9 %all-to-all-start = ((bf16[64,2,4224]{2,1,0:T(2,128)(2,1)}), bf16[64,2,4224]{2,1,0:T(2,128)(2,1)S(1)}, u32[]{:S(2)}, u32[]{:S(2)}) async-start(bf16[64,2,4224]{2,1,0:T(2,128)(2,1)} %reshape.338), calls=%async_computation | async-start | bytes 2162688 | tf_op jit(solution)/shard_map/all_to_all | solution.py:196
  547.1 3.1 fusion.131
  552.5 6.3 %copy.171 = bf16[512,4096]{1,0:T(8,128)(2,1)} copy(bf16[512,4096]{0,1:T(8,128)(2,1)} %bitcast.176) | data formatting | bytes 8388608
  558.8 5.1 all-to-all-done
  565.0 3.2 collective-permute-start.22
  (181 shorter events, 89.1 us)
Async XLA Ops:
  7.2 557.3 %copy-start = (bf16[1,4096,128]{2,1,0:T(8,128)(2,1)S(1)}, bf16[1,4096,128]{2,1,0:T(8,128)(2,1)}, u32[]{:S(2)}) copy-start(bf16[1,4096,128]{2,1,0:T(8,128)(2,1)} %param.27) | copy-start | bytes 3145732
  7.2 391.7 %all-gather.2.cloned.1.call-start = ((), (), s32[]{:S(2)}) async-start(), calls=%async_computation.1 | async-start | bytes 8912896 | tf_op jit(solution)/shard_map/all_gather | solution.py:94
  13.6 10.6 %copy-start.15 = (f32[256,32]{0,1:T(8,128)}, f32[256,32]{0,1:T(8,128)S(1)}, u32[]{:S(2)}) copy-start(f32[256,32]{0,1:T(8,128)S(1)} %get-tuple-element.73) | copy-start | bytes 98308
  19.3 9.6 %copy-start.3 = (bf16[256,2048]{0,1:T(8,128)(2,1)}, bf16[256,2048]{0,1:T(8,128)(2,1)S(1)}, u32[]{:S(2)}) copy-start(bf16[256,2048]{0,1:T(8,128)(2,1)S(1)} %copy.146) | copy-start | bytes 3145732
  24.3 37.0 %copy-start.23 = (f32[2,16]{1,0:T(2,128)S(1)}, f32[2,16]{1,0:T(2,128)}, u32[]{:S(2)}) copy-start(f32[2,16]{1,0:T(2,128)} %get-tuple-element.58) | copy-start | bytes 388
  26.3 82.4 %copy-start.9 = (bf16[512,256]{1,0:T(8,128)(2,1)S(1)}, bf16[512,256]{1,0:T(8,128)(2,1)}, u32[]{:S(2)}) copy-start(bf16[512,256]{1,0:T(8,128)(2,1)} %param.21) | copy-start | bytes 786436
  28.8 26.2 %collective-permute-start = (f32[2,16,64,128]{3,2,1,0:T(8,128)S(1)}, f32[2,16,64,128]{3,2,1,0:T(8,128)S(1)}, u32[]{:S(2)}, u32[]{:S(2)}) collective-permute-start(f32[2,16,64,128]{3,2,1,0:T(8,128)S(1)} %fusion.46), channel_id=1, source_target_pairs={{0,2},{2,4},{4,6},{6,8},{8,10},{10,12},{12,14},{14,16},{16,18},{18... | collective-permute-start | bytes 3145736 | tf_op jit(solution)/shard_map/ppermute | solution.py:70
  55.0 54.4 %copy-start.4 = (f32[2,16,64,128]{3,2,1,0:T(8,128)}, f32[2,16,64,128]{3,2,1,0:T(8,128)S(1)}, u32[]{:S(2)}) copy-start(f32[2,16,64,128]{3,2,1,0:T(8,128)S(1)} %collective-permute-done) | copy-start | bytes 3145732
  55.2 27.6 %collective-permute-start.1 = (f32[2,16,64,128]{3,2,1,0:T(8,128)S(1)}, f32[2,16,64,128]{3,2,1,0:T(8,128)S(1)}, u32[]{:S(2)}, u32[]{:S(2)}) collective-permute-start(f32[2,16,64,128]{3,2,1,0:T(8,128)S(1)} %multiply_add_fusion.4), channel_id=1, source_target_pairs={{0,4},{2,6},{4,8},{6,10},{8,12},{10,14},{12,16},{14,18},{16,20},{1... | collective-permute-start | bytes 3145736 | tf_op jit(solution)/shard_map/ppermute | solution.py:70
  61.3 20.9 %collective-permute-start.2 = (f32[2,16]{1,0:T(2,128)S(1)}, f32[2,16]{1,0:T(2,128)S(1)}, u32[]{:S(2)}, u32[]{:S(2)}) collective-permute-start(f32[2,16]{1,0:T(2,128)S(1)} %copy-done.23), channel_id=1, source_target_pairs={{0,2},{2,4},{4,6},{6,8},{8,10},{10,12},{12,14},{14,16},{16,18},{18... | collective-permute-start | bytes 392 | tf_op jit(solution)/shard_map/ppermute | solution.py:70
  82.8 26.6 %copy-start.6 = (f32[2,16,64,128]{3,2,1,0:T(8,128)}, f32[2,16,64,128]{3,2,1,0:T(8,128)S(1)}, u32[]{:S(2)}) copy-start(f32[2,16,64,128]{3,2,1,0:T(8,128)S(1)} %collective-permute-done.1) | copy-start | bytes 3145732
  83.0 42.7 %collective-permute-start.3 = (f32[2,16,64,128]{3,2,1,0:T(8,128)S(1)}, f32[2,16,64,128]{3,2,1,0:T(8,128)}, u32[]{:S(2)}, u32[]{:S(2)}) collective-permute-start(f32[2,16,64,128]{3,2,1,0:T(8,128)S(1)} %multiply_add_fusion.3), channel_id=1, source_target_pairs={{0,8},{2,10},{4,12},{6,14},{8,16},{10,18},{12,20},{14,22},{16,24},... | collective-permute-start | bytes 3145736 | tf_op jit(solution)/shard_map/ppermute | solution.py:70
  122.3 2.3 collective-permute-start.4
  128.1 45.4 %collective-permute-start.5 = (f32[2,16,64,128]{3,2,1,0:T(8,128)}, f32[2,16,64,128]{3,2,1,0:T(8,128)S(1)}, u32[]{:S(2)}, u32[]{:S(2)}) collective-permute-start(f32[2,16,64,128]{3,2,1,0:T(8,128)} %multiply_add_fusion.2), channel_id=1, source_target_pairs={{0,16},{2,18},{4,20},{6,22},{8,24},{10,26},{12,28},{14,30},{16,32}... | collective-permute-start | bytes 3145736 | tf_op jit(solution)/shard_map/ppermute | solution.py:70
  156.2 7.9 %copy-start.10 = (bf16[512,256]{1,0:T(8,128)(2,1)S(1)}, bf16[512,256]{1,0:T(8,128)(2,1)}, u32[]{:S(2)}) copy-start(bf16[512,256]{1,0:T(8,128)(2,1)} %param.21) | copy-start | bytes 786436
  158.4 27.6 %copy-start.16 = (f32[256,32]{0,1:T(8,128)S(1)}, f32[256,32]{0,1:T(8,128)}, u32[]{:S(2)}) copy-start(f32[256,32]{0,1:T(8,128)} %copy-done.15) | copy-start | bytes 98308
  158.5 27.6 %copy-start.20 = (f32[2,16,256]{2,1,0:T(8,128)S(1)}, f32[2,16,256]{2,1,0:T(8,128)}, u32[]{:S(2)}) copy-start(f32[2,16,256]{2,1,0:T(8,128)} %get-tuple-element.78) | copy-start | bytes 98308
  158.5 27.6 %copy-start.21 = (f32[256,2,16]{0,2,1:T(8,128)S(1)}, f32[256,2,16]{0,2,1:T(8,128)}, u32[]{:S(2)}) copy-start(f32[256,2,16]{0,2,1:T(8,128)} %get-tuple-element.76) | copy-start | bytes 98308
  158.5 15.0 %collective-permute-start.6 = (f32[2,16]{1,0:T(2,128)S(1)}, f32[2,16]{1,0:T(2,128)S(1)}, u32[]{:S(2)}, u32[]{:S(2)}) collective-permute-start(f32[2,16]{1,0:T(2,128)S(1)} %get-tuple-element.54), channel_id=1, source_target_pairs={{0,8},{2,10},{4,12},{6,14},{8,16},{10,18},{12,20},{14,22},{16,24},... | collective-permute-start | bytes 392 | tf_op jit(solution)/shard_map/ppermute | solution.py:70
  173.5 12.6 %copy-start.8 = (f32[2,16,64,128]{3,2,1,0:T(8,128)}, f32[2,16,64,128]{3,2,1,0:T(8,128)S(1)}, u32[]{:S(2)}) copy-start(f32[2,16,64,128]{3,2,1,0:T(8,128)S(1)} %collective-permute-done.5) | copy-start | bytes 3145732
  176.2 28.5 %collective-permute-start.7 = (f32[2,16,64,128]{3,2,1,0:T(8,128)}, f32[2,16,64,128]{3,2,1,0:T(8,128)}, u32[]{:S(2)}, u32[]{:S(2)}) collective-permute-start(f32[2,16,64,128]{3,2,1,0:T(8,128)} %multiply_add_fusion.1), channel_id=1, source_target_pairs={{0,32},{2,34},{4,36},{6,38},{8,40},{10,42},{12,44},{14,46},{16,48}... | collective-permute-start | bytes 3145736 | tf_op jit(solution)/shard_map/ppermute | solution.py:70
  186.0 9.3 %copy-start.18 = (pred[256,256]{1,0:T(8,128)(4,1)}, pred[256,256]{1,0:T(8,128)(4,1)S(1)}, u32[]{:S(2)}) copy-start(pred[256,256]{1,0:T(8,128)(4,1)S(1)} %iota_compare_fusion.2) | copy-start | bytes 196612
  186.1 11.1 %copy-start.2 = (bf16[512,2048]{1,0:T(8,128)(2,1)S(1)}, bf16[512,2048]{1,0:T(8,128)(2,1)}, u32[]{:S(2)}) copy-start(bf16[512,2048]{1,0:T(8,128)(2,1)} %param.19) | copy-start | bytes 6291460
  195.4 18.9 %copy-start.14 = (f32[256,32]{0,1:T(8,128)S(1)}, f32[256,32]{0,1:T(8,128)}, u32[]{:S(2)}) copy-start(f32[256,32]{0,1:T(8,128)} %copy-done.13) | copy-start | bytes 98308
  195.4 18.9 %copy-start.19 = (f32[2,16,256]{2,1,0:T(8,128)S(1)}, f32[2,16,256]{2,1,0:T(8,128)}, u32[]{:S(2)}) copy-start(f32[2,16,256]{2,1,0:T(8,128)} %get-tuple-element.81) | copy-start | bytes 98308
  195.4 4.8 collective-permute-start.8
  207.4 24.8 %collective-permute-start.9 = (f32[2,16,64,128]{3,2,1,0:T(8,128)}, f32[2,16,64,128]{3,2,1,0:T(8,128)}, u32[]{:S(2)}, u32[]{:S(2)}) collective-permute-start(f32[2,16,64,128]{3,2,1,0:T(8,128)} %multiply_add_fusion), channel_id=1, source_target_pairs={{0,64},{2,66},{4,68},{6,70},{8,72},{10,74},{12,76},{14,78},{16,80}... | collective-permute-start | bytes 3145736 | tf_op jit(solution)/shard_map/ppermute | solution.py:70
  214.3 17.9 %copy-start.5 = (f32[2,16,64,128]{3,2,1,0:T(8,128)S(1)}, f32[2,16,64,128]{3,2,1,0:T(8,128)}, u32[]{:S(2)}) copy-start(f32[2,16,64,128]{3,2,1,0:T(8,128)} %copy-done.4) | copy-start | bytes 3145732
  214.3 17.9 %copy-start.7 = (f32[2,16,64,128]{3,2,1,0:T(8,128)S(1)}, f32[2,16,64,128]{3,2,1,0:T(8,128)}, u32[]{:S(2)}) copy-start(f32[2,16,64,128]{3,2,1,0:T(8,128)} %copy-done.6) | copy-start | bytes 3145732
  214.3 17.9 %copy-start.12 = (bf16[512,2,128]{2,1,0:T(2,128)(2,1)S(1)}, bf16[512,2,128]{2,1,0:T(2,128)(2,1)}, u32[]{:S(2)}) copy-start(bf16[512,2,128]{2,1,0:T(2,128)(2,1)} %reshape.329) | copy-start | bytes 786436
  214.3 17.9 %copy-start.17 = (f32[512,2,16]{0,2,1:T(8,128)S(1)}, f32[512,2,16]{0,2,1:T(8,128)}, u32[]{:S(2)}) copy-start(f32[512,2,16]{0,2,1:T(8,128)} %bitcast_bitcast_fusion) | copy-start | bytes 196612
  223.7 8.4 %collective-permute-start.10 = (f32[2,16]{1,0:T(2,128)}, f32[2,16]{1,0:T(2,128)S(1)}, u32[]{:S(2)}, u32[]{:S(2)}) collective-permute-start(f32[2,16]{1,0:T(2,128)} %get-tuple-element.50), channel_id=1, source_target_pairs={{0,32},{2,34},{4,36},{6,38},{8,40},{10,42},{12,44},{14,46},{16,48}... | collective-permute-start | bytes 392 | tf_op jit(solution)/shard_map/ppermute | solution.py:70
  257.5 63.0 %collective-permute-start.11 = (bf16[512,2048]{1,0:T(8,128)(2,1)S(1)}, bf16[512,2048]{1,0:T(8,128)(2,1)}, u32[]{:S(2)}, u32[]{:S(2)}) collective-permute-start(bf16[512,2048]{1,0:T(8,128)(2,1)S(1)} %multiply_convert_fusion), channel_id=1, source_target_pairs={{0,2},{2,4},{4,6},{6,0},{8,10},{10,12},{12,14},{14,8},{16,18},{18,... | collective-permute-start | bytes 6291464 | tf_op jit(solution)/shard_map/ppermute | solution.py:99
  257.6 107.9 %collective-permute-start.12 = (bf16[512,2048]{1,0:T(8,128)(2,1)S(1)}, bf16[512,2048]{1,0:T(8,128)(2,1)}, u32[]{:S(2)}, u32[]{:S(2)}) collective-permute-start(bf16[512,2048]{1,0:T(8,128)(2,1)S(1)} %multiply_convert_fusion), channel_id=1, source_target_pairs={{0,4},{2,6},{4,0},{6,2},{8,12},{10,14},{12,8},{14,10},{16,20},{18,... | collective-permute-start | bytes 6291464 | tf_op jit(solution)/shard_map/ppermute | solution.py:99
  258.5 107.0 %collective-permute-start.13 = (bf16[512,2048]{1,0:T(8,128)(2,1)S(1)}, bf16[512,2048]{1,0:T(8,128)(2,1)}, u32[]{:S(2)}, u32[]{:S(2)}) collective-permute-start(bf16[512,2048]{1,0:T(8,128)(2,1)S(1)} %multiply_convert_fusion), channel_id=1, source_target_pairs={{0,6},{2,0},{4,2},{6,4},{8,14},{10,8},{12,10},{14,12},{16,22},{18,... | collective-permute-start | bytes 6291464 | tf_op jit(solution)/shard_map/ppermute | solution.py:99
  261.8 10.5 %collective-permute-start.14 = (bf16[128,2048]{1,0:T(8,128)(2,1)}, bf16[128,2048]{1,0:T(8,128)(2,1)}, u32[]{:S(2)}, u32[]{:S(2)}) collective-permute-start(bf16[128,2048]{1,0:T(8,128)(2,1)} %slice.187), channel_id=1, source_target_pairs={{8,0},{16,8},{24,16},{32,24},{40,32},{48,40},{56,48},{64,56},{72,6... | collective-permute-start | bytes 1572872 | tf_op jit(solution)/shard_map/ppermute | solution.py:108
  263.1 10.7 %collective-permute-start.15 = (bf16[128,2048]{1,0:T(8,128)(2,1)}, bf16[128,2048]{1,0:T(8,128)(2,1)}, u32[]{:S(2)}, u32[]{:S(2)}) collective-permute-start(bf16[128,2048]{1,0:T(8,128)(2,1)} %slice.187), channel_id=1, source_target_pairs={{8,2},{16,10},{24,18},{32,26},{40,34},{48,42},{56,50},{64,58},{72,... | collective-permute-start | bytes 1572872 | tf_op jit(solution)/shard_map/ppermute | solution.py:108
  272.3 3.1 collective-permute-start.16
  273.8 1.6 collective-permute-start.17
  391.4 7.5 %copy-start.11 = (bf16[128,2048]{1,0:T(8,128)(2,1)S(1)}, bf16[128,2048]{1,0:T(8,128)(2,1)}, u32[]{:S(2)}) copy-start(bf16[128,2048]{1,0:T(8,128)(2,1)} %add_add_fusion) | copy-start | bytes 1572868
  422.2 11.4 %copy-start.26 = (s32[64]{0:T(128)S(1)}, s32[64]{0:T(128)}, u32[]{:S(2)}) copy-start(s32[64]{0:T(128)} %param.31) | copy-start | bytes 772
  426.9 12.9 %collective-permute-start.18 = (bf16[2176,1024]{1,0:T(8,128)(2,1)}, bf16[2176,1024]{1,0:T(8,128)(2,1)}, u32[]{:S(2)}, u32[]{:S(2)}) collective-permute-start(bf16[2176,1024]{1,0:T(8,128)(2,1)} %constant_dynamic-slice_fusion.3), channel_id=1, source_target_pairs={{0,1},{1,0},{2,3},{3,2},{4,5},{5,4},{6,7},{7,6},{8,9},{9,8},{10,11... | collective-permute-start | bytes 13369352 | tf_op jit(solution)/shard_map/ppermute | solution.py:86
  445.7 7.5 %copy-start.24 = (s32[64]{0:T(128)S(1)}, s32[64]{0:T(128)}, u32[]{:S(2)}) copy-start(s32[64]{0:T(128)} %param.29) | copy-start | bytes 772
  446.3 31.2 %collective-permute-start.19 = (bf16[640,1024]{1,0:T(8,128)(2,1)S(1)}, bf16[640,1024]{1,0:T(8,128)(2,1)S(1)}, u32[]{:S(2)}, u32[]{:S(2)}) collective-permute-start(bf16[640,1024]{1,0:T(8,128)(2,1)S(1)} %get-tuple-element.64), channel_id=1, source_target_pairs={{0,2},{2,4},{4,6},{6,0},{8,10},{10,12},{12,14},{14,8},{16,18},{18,... | collective-permute-start | bytes 3932168 | tf_op jit(solution)/shard_map/ppermute | solution.py:99
  446.4 60.7 %collective-permute-start.20 = (bf16[640,1024]{1,0:T(8,128)(2,1)S(1)}, bf16[640,1024]{1,0:T(8,128)(2,1)S(1)}, u32[]{:S(2)}, u32[]{:S(2)}) collective-permute-start(bf16[640,1024]{1,0:T(8,128)(2,1)S(1)} %get-tuple-element.63), channel_id=1, source_target_pairs={{0,4},{2,6},{4,0},{6,2},{8,12},{10,14},{12,8},{14,10},{16,20},{18,... | collective-permute-start | bytes 3932168 | tf_op jit(solution)/shard_map/ppermute | solution.py:99
  450.3 56.8 %collective-permute-start.21 = (bf16[640,1024]{1,0:T(8,128)(2,1)S(1)}, bf16[640,1024]{1,0:T(8,128)(2,1)S(1)}, u32[]{:S(2)}, u32[]{:S(2)}) collective-permute-start(bf16[640,1024]{1,0:T(8,128)(2,1)S(1)} %get-tuple-element.62), channel_id=1, source_target_pairs={{0,6},{2,0},{4,2},{6,4},{8,14},{10,8},{12,10},{14,12},{16,22},{18,... | collective-permute-start | bytes 3932168 | tf_op jit(solution)/shard_map/ppermute | solution.py:99
  538.1 25.8 %all-to-all-start = ((bf16[64,2,4224]{2,1,0:T(2,128)(2,1)}), bf16[64,2,4224]{2,1,0:T(2,128)(2,1)S(1)}, u32[]{:S(2)}, u32[]{:S(2)}) async-start(bf16[64,2,4224]{2,1,0:T(2,128)(2,1)} %reshape.338), calls=%async_computation | async-start | bytes 2162688 | tf_op jit(solution)/shard_map/all_to_all | solution.py:196
  565.0 4.1 collective-permute-start.22
  (5 other events, 25.0 us)
Sparse Core Ops, SparseCore 0:
  10.1 98.1 all-gather.1
